TPU v7x, 256 devices: a whole 4x4x8 slice. The times are simulated.
256 devices in a mesh: gx: 32 (over z_hi, x, core), gy: 4 (over y), gz: 2 (over z_lo).
Axes of the slice: x: 4, y: 4, z: 8 (z_hi: 4, z_lo: 2; z = z_hi * 2 + z_lo), core: 2. Of those that a mesh axis runs over, the one named last changes fastest.
Arguments:
- unary: bfloat16 [128, 32, 128, 128], P('gx', 'gy', 'gz'), may hold values from -3 to 3
- compat: float32 [6, 128, 128], replicated, may hold values from -2.5 to 2.5
- saved_first: bfloat16 [6, 128, 32, 128, 128], P(None, 'gx', 'gy', 'gz'), may hold values from 0.25 to 4
- saved_second: bfloat16 [6, 128, 32, 128, 128], P(None, 'gx', 'gy', 'gz'), may hold values from 0.25 to 4
- cotangent: float32 [128, 32, 128, 128], P('gx', 'gy', 'gz'), may hold values from -6 to 6
Outputs:
- grad_unary: float32 [128, 32, 128, 128], P('gx', 'gy', 'gz')
- grad_compat: float32 [6, 128, 128], replicated
All inputs are finite; a program needn't handle non-finite values.
Results may differ from a plain program's by a relative error of at most 0.0084.
Values may be sent and summed in bfloat16 or wider, within the bound.
No kernel may reach another device: no remote copies, remote signals or barrier semaphores. Data moves between devices by JAX's collectives and lax.ppermute only.
A program may use at most 128 MiB of HBM per device.

v0:
```python
import jax
import jax.numpy as jnp
from jax import lax
from jax.sharding import PartitionSpec as P

OPPOSE = (1, 0, 3, 2, 5, 4)


def extended(cells, sides, width):
    for axis, dim in sides:
        count = lax.axis_size(axis)
        ends = count - 1
        head = lax.slice_in_dim(cells, 0, width, axis=dim)
        tail = lax.slice_in_dim(cells, cells.shape[dim] - width, cells.shape[dim], axis=dim)
        cells = jnp.concatenate(
            [
                lax.ppermute(tail, axis, [(i, (i + 1) % count) for i in range(ends)]),
                cells,
                lax.ppermute(head, axis, [((i + 1) % count, i) for i in range(ends)]),
            ],
            axis=dim,
        )
    return cells


def full_product(fields):
    result = fields[0]
    for index in range(1, 6):
        result = result * fields[index]
    return result


def except_products(fields):
    count = len(fields)
    prefix, suffix = [None] * count, [None] * count
    running = None
    for index in range(count):
        prefix[index] = running
        running = fields[index] if running is None else running * fields[index]
    running = None
    for index in reversed(range(count)):
        suffix[index] = running
        running = fields[index] if running is None else running * fields[index]
    result = []
    for index in range(count):
        if prefix[index] is None:
            result.append(suffix[index])
        elif suffix[index] is None:
            result.append(prefix[index])
        else:
            result.append(prefix[index] * suffix[index])
    return result


def send_terms(potential, messages, whole, weights_b):
    labels = potential.shape[-1]
    scaled = potential * whole
    hidden = [scaled / messages[OPPOSE[direction]] for direction in range(6)]
    hidden_b = jnp.stack(hidden).astype(jnp.bfloat16)
    outgoing = jnp.einsum(
        "dxyzk,dkl->dxyzl", hidden_b, weights_b, preferred_element_type=jnp.float32
    )
    totals = jnp.sum(outgoing, axis=-1, keepdims=True)
    normal = outgoing * (labels / totals)
    return (hidden_b, normal, totals)


def trade(low_face, high_face, axis_dim):
    axis = ("gx", "gy", "gz")[axis_dim]
    count = lax.axis_size(axis)
    odd = lax.axis_index(axis) % 2 == 1
    first = lax.ppermute(
        jnp.where(odd, low_face, high_face), axis, [(i, i ^ 1) for i in range(count)]
    )
    if count > 2:
        second = lax.ppermute(
            jnp.where(odd, high_face, low_face),
            axis,
            [(i, i + 1 if i % 2 == 1 else i - 1) for i in range(1, count - 1)],
        )
    else:
        second = jnp.zeros_like(first)
    lower = jnp.where(odd, first, second)
    upper = jnp.where(odd, second, first)
    return (lower, upper)


def spread(normal_b, lower_edge, upper_edge):
    result = []
    for axis_dim in range(3):
        plus = normal_b[2 * axis_dim]
        minus = normal_b[2 * axis_dim + 1]
        length = plus.shape[axis_dim]
        lower, upper = trade(
            lax.slice_in_dim(minus, 0, 1, axis=axis_dim),
            lax.slice_in_dim(plus, length - 1, length, axis=axis_dim),
            axis_dim,
        )
        ones = jnp.ones_like(lower)
        lower = jnp.where(lower_edge[axis_dim], ones, lower)
        upper = jnp.where(upper_edge[axis_dim], ones, upper)
        result.append(
            jnp.concatenate(
                [lower, lax.slice_in_dim(plus, 0, length - 1, axis=axis_dim)], axis=axis_dim
            )
        )
        result.append(
            jnp.concatenate(
                [lax.slice_in_dim(minus, 1, length, axis=axis_dim), upper], axis=axis_dim
            )
        )
    return result


def gather_back(grad_b):
    result = []
    for axis_dim in range(3):
        plus = grad_b[2 * axis_dim]
        minus = grad_b[2 * axis_dim + 1]
        length = plus.shape[axis_dim]
        lower, upper = trade(
            lax.slice_in_dim(plus, 0, 1, axis=axis_dim),
            lax.slice_in_dim(minus, length - 1, length, axis=axis_dim),
            axis_dim,
        )
        result.append(
            jnp.concatenate(
                [lax.slice_in_dim(plus, 1, length, axis=axis_dim), upper], axis=axis_dim
            )
        )
        result.append(
            jnp.concatenate(
                [lower, lax.slice_in_dim(minus, 0, length - 1, axis=axis_dim)], axis=axis_dim
            )
        )
    return jnp.stack(result).astype(jnp.float32)


def belief_adjoint(potential, arriving, cotangent):
    labels = potential.shape[-1]
    whole = full_product(arriving)
    joint = potential * whole
    summed = jnp.sum(joint, axis=-1, keepdims=True)
    inverse = 1.0 / summed
    belief = joint * inverse
    grad_joint = labels * (cotangent - jnp.sum(cotangent * belief, axis=-1, keepdims=True)) * inverse
    grad_potential = grad_joint * whole
    scaled = grad_joint * potential
    others = except_products(arriving)
    grad_arriving = [(scaled * others[edge]).astype(jnp.bfloat16) for edge in range(6)]
    return (grad_arriving, grad_potential)


def local_adjoint(grad_normal, normal, totals, hidden_b, weights_b):
    labels = normal.shape[-1]
    inner = jnp.sum(grad_normal * normal, axis=-1, keepdims=True)
    grad_out = (labels / totals * (grad_normal - inner / labels)).astype(jnp.bfloat16)
    grad_weights = jnp.einsum(
        "dxyzk,dxyzl->dkl", hidden_b, grad_out, preferred_element_type=jnp.float32
    )
    grad_hidden = jnp.einsum(
        "dxyzl,dkl->dxyzk", grad_out, weights_b, preferred_element_type=jnp.float32
    )
    return (grad_weights, grad_hidden)


def adjoint_terms(grad_hidden, potential, messages, whole):
    ratios = [grad_hidden[OPPOSE[index]] / messages[index] for index in range(6)]
    total = ratios[0]
    for index in range(1, 6):
        total = total + ratios[index]
    unary_term = whole * total
    scaled = potential * whole
    grad_messages = []
    for edge in range(6):
        partial_sum = None
        for index in range(6):
            if index == edge:
                continue
            partial_sum = ratios[index] if partial_sum is None else partial_sum + ratios[index]
        grad_messages.append((partial_sum * (scaled / messages[edge])).astype(jnp.bfloat16))
    return (unary_term, grad_messages)


def all_sum(value, scale, axes):
    count = 1
    for axis in axes:
        count *= lax.axis_size(axis)
    rows = value.reshape(count, -1)
    mine = jnp.sum(lax.all_to_all(rows, axes, 0, 0, tiled=True), axis=0, keepdims=True)
    own = lax.dynamic_slice_in_dim(scale.reshape(count, -1), lax.axis_index(axes), 1, axis=0)
    spread_out = jnp.broadcast_to(own * mine, rows.shape)
    return lax.all_to_all(spread_out, axes, 0, 0, tiled=True).reshape(value.shape)


def body(unary, compat, saved_first, saved_second, cotangent):
    potential = jnp.exp(unary.astype(jnp.float32))
    weights = jnp.exp(compat)
    weights_b = weights.astype(jnp.bfloat16)
    lower_edge = (lax.axis_index("gx") == 0, lax.axis_index("gy") == 0, lax.axis_index("gz") == 0)
    upper_edge = (
        lax.axis_index("gx") == lax.axis_size("gx") - 1,
        lax.axis_index("gy") == lax.axis_size("gy") - 1,
        lax.axis_index("gz") == lax.axis_size("gz") - 1,
    )
    first = [saved_first[index].astype(jnp.float32) for index in range(6)]
    second = [saved_second[index].astype(jnp.float32) for index in range(6)]
    whole_two = full_product(second)
    hidden_two, normal_two, totals_two = send_terms(potential, second, whole_two, weights_b)
    arriving = spread(
        [normal_two[index].astype(jnp.bfloat16) for index in range(6)], lower_edge, upper_edge
    )
    arriving = [value.astype(jnp.float32) for value in arriving]
    grad_arriving, grad_potential = belief_adjoint(potential, arriving, cotangent)
    grad_normal_two = gather_back(grad_arriving)
    weights_two, grad_hidden_two = local_adjoint(
        grad_normal_two, normal_two, totals_two, hidden_two, weights_b
    )
    unary_two, grad_second = adjoint_terms(grad_hidden_two, potential, second, whole_two)
    grad_potential = grad_potential + unary_two
    whole_one = full_product(first)
    hidden_one, normal_one, totals_one = send_terms(potential, first, whole_one, weights_b)
    grad_normal_one = gather_back(grad_second)
    weights_one, grad_hidden_one = local_adjoint(
        grad_normal_one, normal_one, totals_one, hidden_one, weights_b
    )
    ratios_one = [grad_hidden_one[OPPOSE[index]] / first[index] for index in range(6)]
    total_one = ratios_one[0]
    for index in range(1, 6):
        total_one = total_one + ratios_one[index]
    grad_potential = grad_potential + whole_one * total_one
    grad_unary = potential * grad_potential
    grad_compat = all_sum(weights_two + weights_one, weights, ("gx", "gy", "gz"))
    return (grad_unary, grad_compat)


def solution(mesh):
    placed = (
        P("gx", "gy", "gz", None),
        P(),
        P(None, "gx", "gy", "gz", None),
        P(None, "gx", "gy", "gz", None),
        P("gx", "gy", "gz", None),
    )
    return jax.shard_map(
        body,
        mesh=mesh,
        in_specs=placed,
        out_specs=(P("gx", "gy", "gz", None), P()),
        check_vma=False,
    )
```

profile of v0, /device:TPU:1, one launch (start us, length us, event | category | flops | bytes accessed | tf_op | source)
XLA Modules:
  0.0 182.7 jit_solution(1897281257120100827)
XLA Ops:
  0.7 4.7 %bitcast_dynamic-update-slice_fusion.5 = (bf16[6,4,8,64,128]{4,3,2,1,0:T(8,128)(2,1)S(1)}, f32[4,8,64,128]{3,2,1,0:T(8,128)S(1)}, bf16[6,4,8,64,128]{4,3,2,1,0:T(8,128)(2,1)S(1)}, f32[4,8,64,128]{3,2,1,0:T(8,128)S(1)}) fusion(bf16[6,4,8,64,128]{4,3,2,1,0:T(8,128)(2,1)} %param.7, bf16[4,8,64,128]{3,2,1,0:T(8,128)(2,1)} %param.5, ...), kind=kLoop, calls=%fused_computation.155 | loop fusion | flops 7602174 | bytes 9961472
  6.3 1.2 copy-done.5
  8.4 0.3 copy-done.27
  8.7 0.8 fusion.83
  9.5 0.4 bitcast_dynamic-update-slice_fusion
  10.0 1.6 copy-done.16
  11.6 1.9 %fusion.84 = (f32[6,4,8,64]{3,2,1,0:T(8,128)S(1)}, f32[6,4,8,64,128]{4,3,2,1,0:T(8,128)S(1)}) fusion(bf16[6,4,8,64,128]{4,3,2,1,0:T(8,128)(2,1)S(1)} %get-tuple-element.69, bf16[6,128,128]{2,1,0:T(8,128)(2,1)S(1)} %get-tuple-element.42), kind=kOutput, calls=%fused_computation.220 | convolution fusion | flops 404213760 | bytes 9682944 | tf_op jit(solution)/shard_map/dxyzk,dkl->dxyzl/dot_general | solution.py:60
  13.5 2.0 %multiply_convert_fusion = bf16[6,4,8,64,128]{4,3,2,1,0:T(8,128)(2,1)S(1)} fusion(f32[6,4,8,64,128]{4,3,2,1,0:T(8,128)S(1)} %get-tuple-element.64, f32[6,4,8,64]{3,2,1,0:T(8,128)S(1)} %broadcast_divide_fusion.1), kind=kLoop, calls=%fused_computation.11 | loop fusion | flops 3145728 | bytes 9486336 | tf_op jit(solution)/shard_map/convert.29
  15.5 0.6 copy-done.3
  16.1 1.1 slice_bitcast_fusion.13
  17.3 0.8 copy-done.11
  18.1 2.6 %collective-permute-start.4 = (bf16[4,8,1,128]{3,2,1,0:T(2,128)(2,1)S(1)}, bf16[4,8,1,128]{3,2,1,0:T(2,128)(2,1)S(1)}, u32[]{:S(2)}, u32[]{:S(2)}) collective-permute-start(bf16[4,8,1,128]{3,2,1,0:T(2,128)(2,1)S(1)} %broadcast_select_fusion.27), channel_id=1, source_target_pairs={{0,1},{1,0},{2,3},{3,2},{4,5},{5,4},{6,7},{7,6},{8,9},{9,8},{10,11... | collective-permute-start | bytes 24584 | tf_op jit(solution)/shard_map/ppermute | solution.py:72
  20.6 1.7 select_bitcast_fusion.1
  22.3 1.0 collective-permute-start
  23.3 3.0 %collective-permute-start.1 = (bf16[1,8,64,128]{3,2,1,0:T(8,128)(2,1)}, bf16[1,8,64,128]{3,2,1,0:T(8,128)(2,1)}, u32[]{:S(2)}, u32[]{:S(2)}) collective-permute-start(bf16[1,8,64,128]{3,2,1,0:T(8,128)(2,1)} %get-tuple-element.26), channel_id=1, source_target_pairs={{8,16},{16,8},{24,32},{32,24},{40,48},{48,40},{56,64},{64,56},{72,... | collective-permute-start | bytes 393224 | tf_op jit(solution)/shard_map/ppermute | solution.py:76
  26.3 1.5 broadcast_select_fusion.17
  27.8 1.3 collective-permute-start.2
  29.1 1.3 collective-permute-start.3
  30.4 1.9 %slice_bitcast_fusion.17 = (bf16[3,8,64,128]{3,2,1,0:T(8,128)(2,1)}, bf16[3,8,64,128]{3,2,1,0:T(8,128)(2,1)S(1)}) fusion(bf16[6,4,8,64,128]{4,3,2,1,0:T(8,128)(2,1)} %copy-done.11), kind=kLoop, calls=%fused_computation.165 | loop fusion | bytes 1572864 | tf_op jit(solution)/shard_map/slice | solution.py:104
  32.3 6.3 %fusion.85 = (f32[6,4,8,64]{3,2,1,0:T(8,128)S(1)}, f32[6,4,8,64,128]{4,3,2,1,0:T(8,128)}) fusion(bf16[6,4,8,64,128]{4,3,2,1,0:T(8,128)(2,1)} %copy-done.16, bf16[6,128,128]{2,1,0:T(8,128)(2,1)S(1)} %get-tuple-element.42), kind=kOutput, calls=%fused_computation.221 | convolution fusion | flops 404213760 | bytes 9682944 | tf_op jit(solution)/shard_map/dxyzk,dkl->dxyzl/dot_general | solution.py:60
  38.6 0.7 broadcast_divide_fusion
  39.4 1.2 slice.286
  40.7 1.1 slice.287
  41.9 1.0 select_select_fusion.3
  42.9 1.0 select_select_fusion.1
  43.9 1.9 %fusion.78 = (f32[4,8,64]{2,1,0:T(8,128)S(1)}, f32[4,8,64,128]{3,2,1,0:T(8,128)S(1)}) fusion(bf16[4,8,64,128]{3,2,1,0:T(8,128)(2,1)} %param.5, bf16[4,8,1,128]{3,2,1,0:T(2,128)(2,1)S(1)} %get-tuple-element.62, bf16[4,8,63,128]{3,2,1,0:T(8,128)(2,1)S(1)} %slice.293, bf16[4,8,63,128]{3,2,1,0:T(8,128)(2,1)S(1)} %bitcast.366, ...), kind=kLoop, calls=%fused_computation.218 | loop fusion | flops 8386560 | bytes 4726784 | tf_op jit(solution)/shard_map/reduce_sum | solution.py:143
  45.8 11.2 %fusion.35 = (bf16[4,8,64,128]{3,2,1,0:T(8,128)(2,1)S(1)}, f32[4,8,64,128]{3,2,1,0:T(8,128)S(1)}, f32[4,8,64,128]{3,2,1,0:T(8,128)}) fusion(bf16[4,1,64,128]{3,2,1,0:T(8,128)(2,1)S(1)} %get-tuple-element.54, bf16[4,7,64,128]{3,2,1,0:T(8,128)(2,1)S(1)} %slice.287, bf16[4,7,64,128]{3,2,1,0:T(8,128)(2,1)S(1)} %slice.286, ...), kind=kOutput, calls=%fused_computation.73 | output fusion | flops 10225791 | bytes 7880704 | tf_op jit(solution)/shard_map/sub | solution.py:146
  57.0 0.8 multiply_convert_fusion.7
  57.8 0.6 multiply_convert_fusion.9
  58.5 0.7 fusion.31
  59.1 0.7 fusion.33
  60.3 0.8 collective-permute-start.7
  61.1 4.6 %collective-permute-start.8 = (bf16[4,1,64,128]{3,2,1,0:T(8,128)(2,1)S(1)}, bf16[4,1,64,128]{3,2,1,0:T(8,128)(2,1)S(1)}, u32[]{:S(2)}, u32[]{:S(2)}) collective-permute-start(bf16[4,1,64,128]{3,2,1,0:T(8,128)(2,1)S(1)} %get-tuple-element.33), channel_id=1, source_target_pairs={{0,2},{2,0},{4,6},{6,4},{1,3},{3,1},{5,7},{7,5},{8,10},{10,8},{12,... | collective-permute-start | bytes 196616 | tf_op jit(solution)/shard_map/ppermute | solution.py:72
  65.7 4.6 %collective-permute-start.5 = (bf16[1,8,64,128]{3,2,1,0:T(8,128)(2,1)S(1)}, bf16[1,8,64,128]{3,2,1,0:T(8,128)(2,1)S(1)}, u32[]{:S(2)}, u32[]{:S(2)}) collective-permute-start(bf16[1,8,64,128]{3,2,1,0:T(8,128)(2,1)S(1)} %get-tuple-element.36), channel_id=1, source_target_pairs={{8,16},{16,8},{24,32},{32,24},{40,48},{48,40},{56,64},{64,56},{72,... | collective-permute-start | bytes 393224 | tf_op jit(solution)/shard_map/ppermute | solution.py:76
  70.4 0.3 collective-permute-start.6
  70.8 2.2 %collective-permute-done.5 = bf16[1,8,64,128]{3,2,1,0:T(8,128)(2,1)S(1)} collective-permute-done((bf16[1,8,64,128]{3,2,1,0:T(8,128)(2,1)S(1)}, bf16[1,8,64,128]{3,2,1,0:T(8,128)(2,1)S(1)}, u32[]{:S(2)}, u32[]{:S(2)}) %collective-permute-start.5) | collective-permute-done | bytes 131104 | tf_op jit(solution)/shard_map/ppermute | solution.py:76
  73.4 0.2 fusion.60
  73.7 3.8 %fusion.1 = f32[6,4,8,64]{3,2,1,0:T(8,128)S(1)} fusion(bf16[6,4,8,64,128]{4,3,2,1,0:T(8,128)(2,1)S(1)} %fusion.60, f32[6,4,8,64,128]{4,3,2,1,0:T(8,128)S(1)} %bitcast.363, f32[6,4,8,64]{3,2,1,0:T(8,128)S(1)} %broadcast_divide_fusion.1), kind=kLoop, calls=%fused_computation.5 | loop fusion | flops 6279168 | bytes 9535488 | tf_op jit(solution)/shard_map/reduce_sum | solution.py:156
  77.5 5.7 %fusion.15 = f32[6,128,128]{2,1,0:T(8,128)S(1)} fusion(bf16[6,4,8,64,128]{4,3,2,1,0:T(8,128)(2,1)S(1)} %copy-done.19, bf16[6,4,8,64,128]{4,3,2,1,0:T(8,128)(2,1)S(1)} %fusion.60, f32[6,4,8,64]{3,2,1,0:T(8,128)S(1)} %broadcast_multiply_fusion.1, f32[6,4,8,64]{3,2,1,0:T(8,128)S(1)} %broadcast_divide_fusion.1), kind=kOutput, calls=%fused_computation.65 | convolution fusion | flops 408944640 | bytes 6782976 | tf_op jit(solution)/shard_map/dxyzk,dxyzl->dkl/dot_general | solution.py:158
  83.2 5.5 %fusion.72 = f32[6,4,8,64,128]{4,3,2,1,0:T(8,128)S(1)} fusion(bf16[6,128,128]{2,1,0:T(8,128)(2,1)S(1)} %copy-done.15, bf16[6,4,8,64,128]{4,3,2,1,0:T(8,128)(2,1)S(1)} %fusion.60, f32[6,4,8,64]{3,2,1,0:T(8,128)S(1)} %broadcast_multiply_fusion.1, f32[6,4,8,64]{3,2,1,0:T(8,128)S(1)} %broadcast_divide_fusion.1), kind=kOutput, calls=%fused_computation.170 | convolution fusion | flops 408944640 | bytes 9732096 | tf_op jit(solution)/shard_map/dxyzl,dkl->dxyzk/dot_general | solution.py:161
  88.8 1.1 multiply_convert_fusion.2
  89.9 0.5 multiply_convert_fusion.1
  90.4 0.4 collective-permute-start.14
  90.8 1.0 multiply_convert_fusion.6
  91.8 1.2 multiply_convert_fusion.3
  93.4 0.8 collective-permute-start.12
  94.2 2.9 %collective-permute-start.13 = (bf16[4,1,64,128]{3,2,1,0:T(8,128)(2,1)S(1)}, bf16[4,1,64,128]{3,2,1,0:T(8,128)(2,1)S(1)}, u32[]{:S(2)}, u32[]{:S(2)}) collective-permute-start(bf16[4,1,64,128]{3,2,1,0:T(8,128)(2,1)S(1)} %get-tuple-element.27), channel_id=1, source_target_pairs={{0,2},{2,0},{4,6},{6,4},{1,3},{3,1},{5,7},{7,5},{8,10},{10,8},{12,... | collective-permute-start | bytes 196616 | tf_op jit(solution)/shard_map/ppermute | solution.py:72
  97.1 4.5 %collective-permute-start.10 = (bf16[1,8,64,128]{3,2,1,0:T(8,128)(2,1)S(1)}, bf16[1,8,64,128]{3,2,1,0:T(8,128)(2,1)S(1)}, u32[]{:S(2)}, u32[]{:S(2)}) collective-permute-start(bf16[1,8,64,128]{3,2,1,0:T(8,128)(2,1)S(1)} %get-tuple-element.30), channel_id=1, source_target_pairs={{8,16},{16,8},{24,32},{32,24},{40,48},{48,40},{56,64},{64,56},{72,... | collective-permute-start | bytes 393224 | tf_op jit(solution)/shard_map/ppermute | solution.py:76
  101.8 2.4 %collective-permute-done.10 = bf16[1,8,64,128]{3,2,1,0:T(8,128)(2,1)S(1)} collective-permute-done((bf16[1,8,64,128]{3,2,1,0:T(8,128)(2,1)S(1)}, bf16[1,8,64,128]{3,2,1,0:T(8,128)(2,1)S(1)}, u32[]{:S(2)}, u32[]{:S(2)}) %collective-permute-start.10) | collective-permute-done | bytes 131104 | tf_op jit(solution)/shard_map/ppermute | solution.py:76
  104.7 0.2 fusion.66
  105.0 0.2 copy-done.26
  105.2 3.8 %fusion.4 = f32[6,4,8,64]{3,2,1,0:T(8,128)S(1)} fusion(bf16[6,4,8,64,128]{4,3,2,1,0:T(8,128)(2,1)S(1)} %fusion.66, f32[6,4,8,64,128]{4,3,2,1,0:T(8,128)S(1)} %bitcast.365, f32[6,4,8,64]{3,2,1,0:T(8,128)S(1)} %copy-done.26), kind=kLoop, calls=%fused_computation.8 | loop fusion | flops 6279168 | bytes 9535488 | tf_op jit(solution)/shard_map/reduce_sum | solution.py:156
  109.1 6.3 %fusion.25 = f32[6,128,128]{2,1,0:T(8,128)} fusion(f32[6,128,128]{2,1,0:T(8,128)S(1)} %fusion.15, bf16[6,4,8,64,128]{4,3,2,1,0:T(8,128)(2,1)S(1)} %copy-done.17, bf16[6,4,8,64,128]{4,3,2,1,0:T(8,128)(2,1)S(1)} %fusion.66, f32[6,4,8,64]{3,2,1,0:T(8,128)S(1)} %broadcast_multiply_fusion, f32[6,4,8,64]{3,2,1,0:T(8,128)S(1)} %copy-done.26), kind=kOutput, calls=%fused_computation.67 | convolution fusion | flops 409042944 | bytes 7176192 | tf_op jit(solution)/shard_map/dxyzk,dxyzl->dkl/dot_general | solution.py:158
  115.4 21.8 %all-to-all-start = ((f32[256,1,384]{2,1,0:T(1,128)}), f32[256,1,384]{2,1,0:T(1,128)}, u32[]{:S(2)}, u32[]{:S(2)}) async-start(f32[256,1,384]{2,1,0:T(1,128)} %bitcast.75), calls=%async_computation | async-start | bytes 786432 | tf_op jit(solution)/shard_map/all_to_all | solution.py:190
  137.2 0.8 reshape.80
  138.0 7.3 %fusion.68 = f32[6,4,8,64,128]{4,3,2,1,0:T(8,128)} fusion(bf16[6,128,128]{2,1,0:T(8,128)(2,1)S(1)} %copy-done.15, bf16[6,4,8,64,128]{4,3,2,1,0:T(8,128)(2,1)} %copy-done.9, f32[6,4,8,64]{3,2,1,0:T(8,128)S(1)} %broadcast_multiply_fusion, f32[6,4,8,64]{3,2,1,0:T(8,128)S(1)} %copy-done.26), kind=kOutput, calls=%fused_computation.166 | convolution fusion | flops 408944640 | bytes 9732096 | tf_op jit(solution)/shard_map/dxyzl,dkl->dxyzk/dot_general | solution.py:161
  145.3 9.4 %all-to-all-done = f32[256,1,384]{2,1,0:T(1,128)} async-done(((f32[256,1,384]{2,1,0:T(1,128)}), f32[256,1,384]{2,1,0:T(1,128)}, u32[]{:S(2)}, u32[]{:S(2)}) %all-to-all-start) | async-done | bytes 393248 | tf_op jit(solution)/shard_map/all_to_all | solution.py:190
  154.7 1.3 reduce_sum.69
  156.0 0.7 multiply_reduce_fusion
  156.7 1.0 broadcast_in_dim.27
  157.7 5.8 %all-to-all-start.1 = ((f32[256,1,384]{2,1,0:T(1,128)}), f32[256,1,384]{2,1,0:T(1,128)S(1)}, u32[]{:S(2)}, u32[]{:S(2)}) async-start(f32[256,1,384]{2,1,0:T(1,128)} %broadcast_in_dim.27), calls=%async_computation.1 | async-start | bytes 786432 | tf_op jit(solution)/shard_map/all_to_all | solution.py:193
  163.5 7.6 %fusion.44 = f32[4,8,64,128]{3,2,1,0:T(8,128)} fusion(f32[6,4,8,64,128]{4,3,2,1,0:T(8,128)} %fusion.68, f32[4,8,64,128]{3,2,1,0:T(8,128)} %copy-done.6, f32[4,8,64,128]{3,2,1,0:T(8,128)} %get-tuple-element.65, bf16[4,8,64,128]{3,2,1,0:T(8,128)(2,1)} %param.5, f32[4,8,64,128]{3,2,1,0:T(8,128)} %copy-done.8, f32[4,8,64,128]{3,2,1,0:T(8,128)} %copy-done.12, ...), kind=kLoop, calls=%fused_computation.82 | loop fusion | flops 12320768 | bytes 19922944 | tf_op jit(solution)/shard_map/mul | solution.py:232
  171.0 10.9 %all-to-all-done.1 = f32[256,1,384]{2,1,0:T(1,128)S(1)} async-done(((f32[256,1,384]{2,1,0:T(1,128)}), f32[256,1,384]{2,1,0:T(1,128)S(1)}, u32[]{:S(2)}, u32[]{:S(2)}) %all-to-all-start.1) | async-done | bytes 393248 | tf_op jit(solution)/shard_map/all_to_all | solution.py:193
  181.9 0.7 copy.56
  (125 shorter events, 3.9 us)
Async XLA Ops:
  0.6 4.7 %copy-start = (bf16[6,4,8,64,128]{4,3,2,1,0:T(8,128)(2,1)S(1)}, bf16[6,4,8,64,128]{4,3,2,1,0:T(8,128)(2,1)}, u32[]{:S(2)}) copy-start(bf16[6,4,8,64,128]{4,3,2,1,0:T(8,128)(2,1)} %param.8) | copy-start | bytes 9437188
  5.6 1.9 %copy-start.5 = (bf16[6,4,8,64,128]{4,3,2,1,0:T(8,128)(2,1)S(1)}, bf16[6,4,8,64,128]{4,3,2,1,0:T(8,128)(2,1)}, u32[]{:S(2)}) copy-start(bf16[6,4,8,64,128]{4,3,2,1,0:T(8,128)(2,1)} %param.7) | copy-start | bytes 9437188
  7.7 1.0 copy-start.27
  9.5 22.8 %copy-start.14 = (bf16[6,128,128]{2,1,0:T(8,128)(2,1)}, bf16[6,128,128]{2,1,0:T(8,128)(2,1)S(1)}, u32[]{:S(2)}) copy-start(bf16[6,128,128]{2,1,0:T(8,128)(2,1)S(1)} %get-tuple-element.42) | copy-start | bytes 589828
  10.0 1.6 copy-start.16
  10.0 3.5 %copy-start.18 = (bf16[6,4,8,64,128]{4,3,2,1,0:T(8,128)(2,1)}, bf16[6,4,8,64,128]{4,3,2,1,0:T(8,128)(2,1)S(1)}, u32[]{:S(2)}) copy-start(bf16[6,4,8,64,128]{4,3,2,1,0:T(8,128)(2,1)S(1)} %get-tuple-element.69) | copy-start | bytes 9437188
  13.5 2.6 %copy-start.3 = (f32[6,4,8,64,128]{4,3,2,1,0:T(8,128)}, f32[6,4,8,64,128]{4,3,2,1,0:T(8,128)S(1)}, u32[]{:S(2)}) copy-start(f32[6,4,8,64,128]{4,3,2,1,0:T(8,128)S(1)} %get-tuple-element.64) | copy-start | bytes 18874372
  16.1 1.9 %copy-start.11 = (bf16[6,4,8,64,128]{4,3,2,1,0:T(8,128)(2,1)}, bf16[6,4,8,64,128]{4,3,2,1,0:T(8,128)(2,1)S(1)}, u32[]{:S(2)}) copy-start(bf16[6,4,8,64,128]{4,3,2,1,0:T(8,128)(2,1)S(1)} %multiply_convert_fusion) | copy-start | bytes 9437188
  18.0 11.1 %copy-start.22 = (bf16[4,8,64,128]{3,2,1,0:T(8,128)(2,1)}, bf16[4,8,64,128]{3,2,1,0:T(8,128)(2,1)S(1)}, u32[]{:S(2)}) copy-start(bf16[4,8,64,128]{3,2,1,0:T(8,128)(2,1)S(1)} %get-tuple-element.22) | copy-start | bytes 1572868
  18.1 23.7 %collective-permute-start.4 = (bf16[4,8,1,128]{3,2,1,0:T(2,128)(2,1)S(1)}, bf16[4,8,1,128]{3,2,1,0:T(2,128)(2,1)S(1)}, u32[]{:S(2)}, u32[]{:S(2)}) collective-permute-start(bf16[4,8,1,128]{3,2,1,0:T(2,128)(2,1)S(1)} %broadcast_select_fusion.27), channel_id=1, source_target_pairs={{0,1},{1,0},{2,3},{3,2},{4,5},{5,4},{6,7},{7,6},{8,9},{9,8},{10,11... | collective-permute-start | bytes 24584 | tf_op jit(solution)/shard_map/ppermute | solution.py:72
  22.3 20.6 %collective-permute-start = (bf16[1,8,64,128]{3,2,1,0:T(8,128)(2,1)}, bf16[1,8,64,128]{3,2,1,0:T(8,128)(2,1)}, u32[]{:S(2)}, u32[]{:S(2)}) collective-permute-start(bf16[1,8,64,128]{3,2,1,0:T(8,128)(2,1)} %get-tuple-element.25), channel_id=1, source_target_pairs={{0,8},{8,0},{16,24},{24,16},{32,40},{40,32},{48,56},{56,48},{64,72... | collective-permute-start | bytes 393224 | tf_op jit(solution)/shard_map/ppermute | solution.py:72
  23.3 19.6 %collective-permute-start.1 = (bf16[1,8,64,128]{3,2,1,0:T(8,128)(2,1)}, bf16[1,8,64,128]{3,2,1,0:T(8,128)(2,1)}, u32[]{:S(2)}, u32[]{:S(2)}) collective-permute-start(bf16[1,8,64,128]{3,2,1,0:T(8,128)(2,1)} %get-tuple-element.26), channel_id=1, source_target_pairs={{8,16},{16,8},{24,32},{32,24},{40,48},{48,40},{56,64},{64,56},{72,... | collective-permute-start | bytes 393224 | tf_op jit(solution)/shard_map/ppermute | solution.py:76
  27.8 14.0 %collective-permute-start.2 = (bf16[4,1,64,128]{3,2,1,0:T(8,128)(2,1)}, bf16[4,1,64,128]{3,2,1,0:T(8,128)(2,1)}, u32[]{:S(2)}, u32[]{:S(2)}) collective-permute-start(bf16[4,1,64,128]{3,2,1,0:T(8,128)(2,1)} %get-tuple-element.37), channel_id=1, source_target_pairs={{0,2},{2,0},{4,6},{6,4},{1,3},{3,1},{5,7},{7,5},{8,10},{10,8},{12,... | collective-permute-start | bytes 196616 | tf_op jit(solution)/shard_map/ppermute | solution.py:72
  29.1 12.7 %collective-permute-start.3 = (bf16[4,1,64,128]{3,2,1,0:T(8,128)(2,1)}, bf16[4,1,64,128]{3,2,1,0:T(8,128)(2,1)}, u32[]{:S(2)}, u32[]{:S(2)}) collective-permute-start(bf16[4,1,64,128]{3,2,1,0:T(8,128)(2,1)} %get-tuple-element.38), channel_id=1, source_target_pairs={{2,4},{4,2},{3,5},{5,3},{10,12},{12,10},{11,13},{13,11},{18,20},{2... | collective-permute-start | bytes 196616 | tf_op jit(solution)/shard_map/ppermute | solution.py:76
  39.4 19.7 %copy-start.4 = (bf16[4,8,63,128]{3,2,1,0:T(8,128)(2,1)}, bf16[4,8,63,128]{3,2,1,0:T(8,128)(2,1)S(1)}, u32[]{:S(2)}) copy-start(bf16[4,8,63,128]{3,2,1,0:T(8,128)(2,1)S(1)} %slice.293) | copy-start | bytes 1548292
  41.7 4.1 %copy-start.10 = (bf16[3,8,64,128]{3,2,1,0:T(8,128)(2,1)S(1)}, bf16[3,8,64,128]{3,2,1,0:T(8,128)(2,1)}, u32[]{:S(2)}) copy-start(bf16[3,8,64,128]{3,2,1,0:T(8,128)(2,1)} %get-tuple-element.23) | copy-start | bytes 1179652
  41.8 4.1 %copy-start.13 = (bf16[4,8,64,128]{3,2,1,0:T(8,128)(2,1)S(1)}, bf16[4,8,64,128]{3,2,1,0:T(8,128)(2,1)}, u32[]{:S(2)}) copy-start(bf16[4,8,64,128]{3,2,1,0:T(8,128)(2,1)} %param.5) | copy-start | bytes 1572868
  41.8 4.1 %copy-start.25 = (f32[4,8,64,128]{3,2,1,0:T(8,128)S(1)}, f32[4,8,64,128]{3,2,1,0:T(8,128)}, u32[]{:S(2)}) copy-start(f32[4,8,64,128]{3,2,1,0:T(8,128)} %param.9) | copy-start | bytes 3145732
  45.8 11.3 %copy-start.8 = (f32[4,8,64,128]{3,2,1,0:T(8,128)}, f32[4,8,64,128]{3,2,1,0:T(8,128)S(1)}, u32[]{:S(2)}) copy-start(f32[4,8,64,128]{3,2,1,0:T(8,128)S(1)} %get-tuple-element.13) | copy-start | bytes 3145732
  58.4 1.6 copy-start.23
  59.1 0.9 copy-start.21
  59.1 14.5 %slice-start = ((s8[6291456]{0:T(1024)(128)(4,1)}), s8[4194304]{0:T(1024)(128)(4,1)S(1)}, s32[]{:S(2)}) async-start(s8[6291456]{0:T(1024)(128)(4,1)} %bitcast.362), calls=%async_computation.2 | async-start | bytes 8388608
  59.8 10.8 %collective-permute-start.9 = (bf16[4,8,1,128]{3,2,1,0:T(2,128)(2,1)S(1)}, bf16[4,8,1,128]{3,2,1,0:T(2,128)(2,1)S(1)}, u32[]{:S(2)}, u32[]{:S(2)}) collective-permute-start(bf16[4,8,1,128]{3,2,1,0:T(2,128)(2,1)S(1)} %broadcast_select_fusion.24), channel_id=1, source_target_pairs={{0,1},{1,0},{2,3},{3,2},{4,5},{5,4},{6,7},{7,6},{8,9},{9,8},{10,11... | collective-permute-start | bytes 24584 | tf_op jit(solution)/shard_map/ppermute | solution.py:72
  60.0 13.1 %slice-start.6 = ((bf16[4,8,64,128]{3,2,1,0:T(8,128)(2,1)}), bf16[4,7,64,128]{3,2,1,0:T(8,128)(2,1)S(1)}, s32[]{:S(2)}) async-start(bf16[4,8,64,128]{3,2,1,0:T(8,128)(2,1)} %copy-done.23), calls=%async_computation.8 | async-start | bytes 917504 | tf_op jit(solution)/shard_map/slice | solution.py:128
  60.1 13.0 %slice-start.5 = ((bf16[4,8,64,128]{3,2,1,0:T(8,128)(2,1)}), bf16[3,8,64,128]{3,2,1,0:T(8,128)(2,1)S(1)}, s32[]{:S(2)}) async-start(bf16[4,8,64,128]{3,2,1,0:T(8,128)(2,1)} %copy-done.21), calls=%async_computation.7 | async-start | bytes 786432 | tf_op jit(solution)/shard_map/slice | solution.py:133
  60.1 13.6 %slice-start.1 = ((s8[6291456]{0:T(1024)(128)(4,1)}), s8[2097152]{0:T(1024)(128)(4,1)S(1)}, s32[]{:S(2)}) async-start(s8[6291456]{0:T(1024)(128)(4,1)} %bitcast.362), calls=%async_computation.3 | async-start | bytes 4194304
  60.3 10.4 %collective-permute-start.7 = (bf16[4,1,64,128]{3,2,1,0:T(8,128)(2,1)S(1)}, bf16[4,1,64,128]{3,2,1,0:T(8,128)(2,1)S(1)}, u32[]{:S(2)}, u32[]{:S(2)}) collective-permute-start(bf16[4,1,64,128]{3,2,1,0:T(8,128)(2,1)S(1)} %get-tuple-element.34), channel_id=1, source_target_pairs={{2,4},{4,2},{3,5},{5,3},{10,12},{12,10},{11,13},{13,11},{18,20},{2... | collective-permute-start | bytes 196616 | tf_op jit(solution)/shard_map/ppermute | solution.py:76
  61.1 9.6 %collective-permute-start.8 = (bf16[4,1,64,128]{3,2,1,0:T(8,128)(2,1)S(1)}, bf16[4,1,64,128]{3,2,1,0:T(8,128)(2,1)S(1)}, u32[]{:S(2)}, u32[]{:S(2)}) collective-permute-start(bf16[4,1,64,128]{3,2,1,0:T(8,128)(2,1)S(1)} %get-tuple-element.33), channel_id=1, source_target_pairs={{0,2},{2,0},{4,6},{6,4},{1,3},{3,1},{5,7},{7,5},{8,10},{10,8},{12,... | collective-permute-start | bytes 196616 | tf_op jit(solution)/shard_map/ppermute | solution.py:72
  65.7 7.3 %collective-permute-start.5 = (bf16[1,8,64,128]{3,2,1,0:T(8,128)(2,1)S(1)}, bf16[1,8,64,128]{3,2,1,0:T(8,128)(2,1)S(1)}, u32[]{:S(2)}, u32[]{:S(2)}) collective-permute-start(bf16[1,8,64,128]{3,2,1,0:T(8,128)(2,1)S(1)} %get-tuple-element.36), channel_id=1, source_target_pairs={{8,16},{16,8},{24,32},{32,24},{40,48},{48,40},{56,64},{64,56},{72,... | collective-permute-start | bytes 393224 | tf_op jit(solution)/shard_map/ppermute | solution.py:76
  70.4 2.6 %collective-permute-start.6 = (bf16[1,8,64,128]{3,2,1,0:T(8,128)(2,1)S(1)}, bf16[1,8,64,128]{3,2,1,0:T(8,128)(2,1)S(1)}, u32[]{:S(2)}, u32[]{:S(2)}) collective-permute-start(bf16[1,8,64,128]{3,2,1,0:T(8,128)(2,1)S(1)} %get-tuple-element.35), channel_id=1, source_target_pairs={{0,8},{8,0},{16,24},{24,16},{32,40},{40,32},{48,56},{56,48},{64,72... | collective-permute-start | bytes 393224 | tf_op jit(solution)/shard_map/ppermute | solution.py:72
  73.7 3.8 %copy-start.19 = (bf16[6,4,8,64,128]{4,3,2,1,0:T(8,128)(2,1)S(1)}, bf16[6,4,8,64,128]{4,3,2,1,0:T(8,128)(2,1)}, u32[]{:S(2)}) copy-start(bf16[6,4,8,64,128]{4,3,2,1,0:T(8,128)(2,1)} %copy-done.18) | copy-start | bytes 9437188
  77.5 5.7 %copy-start.15 = (bf16[6,128,128]{2,1,0:T(8,128)(2,1)S(1)}, bf16[6,128,128]{2,1,0:T(8,128)(2,1)}, u32[]{:S(2)}) copy-start(bf16[6,128,128]{2,1,0:T(8,128)(2,1)} %copy-done.14) | copy-start | bytes 589828
  83.2 5.6 %copy-start.1 = (bf16[6,4,8,64,128]{4,3,2,1,0:T(8,128)(2,1)S(1)}, bf16[6,4,8,64,128]{4,3,2,1,0:T(8,128)(2,1)}, u32[]{:S(2)}) copy-start(bf16[6,4,8,64,128]{4,3,2,1,0:T(8,128)(2,1)} %param.8) | copy-start | bytes 9437188
  89.9 1.9 %copy-start.12 = (f32[4,8,64,128]{3,2,1,0:T(8,128)}, f32[4,8,64,128]{3,2,1,0:T(8,128)S(1)}, u32[]{:S(2)}) copy-start(f32[4,8,64,128]{3,2,1,0:T(8,128)S(1)} %get-tuple-element.5) | copy-start | bytes 3145732
  89.9 1.9 %copy-start.6 = (f32[4,8,64,128]{3,2,1,0:T(8,128)}, f32[4,8,64,128]{3,2,1,0:T(8,128)S(1)}, u32[]{:S(2)}) copy-start(f32[4,8,64,128]{3,2,1,0:T(8,128)S(1)} %get-tuple-element.7) | copy-start | bytes 3145732
  90.3 1.5 copy-start.7
  90.4 11.3 %collective-permute-start.14 = (bf16[4,8,1,128]{3,2,1,0:T(2,128)(2,1)S(1)}, bf16[4,8,1,128]{3,2,1,0:T(2,128)(2,1)S(1)}, u32[]{:S(2)}, u32[]{:S(2)}) collective-permute-start(bf16[4,8,1,128]{3,2,1,0:T(2,128)(2,1)S(1)} %broadcast_select_fusion.21), channel_id=1, source_target_pairs={{0,1},{1,0},{2,3},{3,2},{4,5},{5,4},{6,7},{7,6},{8,9},{9,8},{10,11... | collective-permute-start | bytes 24584 | tf_op jit(solution)/shard_map/ppermute | solution.py:72
  91.8 1.3 copy-start.20
  91.8 13.1 %slice-start.2 = ((s8[6291456]{0:T(1024)(128)(4,1)}), s8[2097152]{0:T(1024)(128)(4,1)S(1)}, s32[]{:S(2)}) async-start(s8[6291456]{0:T(1024)(128)(4,1)} %bitcast.364), calls=%async_computation.4 | async-start | bytes 4194304
  93.1 11.9 %slice-start.3 = ((s8[6291456]{0:T(1024)(128)(4,1)}), s8[4194304]{0:T(1024)(128)(4,1)S(1)}, s32[]{:S(2)}) async-start(s8[6291456]{0:T(1024)(128)(4,1)} %bitcast.364), calls=%async_computation.5 | async-start | bytes 8388608
  93.1 11.2 %slice-start.4 = ((bf16[4,8,64,128]{3,2,1,0:T(8,128)(2,1)}), bf16[3,8,64,128]{3,2,1,0:T(8,128)(2,1)S(1)}, s32[]{:S(2)}) async-start(bf16[4,8,64,128]{3,2,1,0:T(8,128)(2,1)} %copy-done.20), calls=%async_computation.6 | async-start | bytes 786432 | tf_op jit(solution)/shard_map/slice | solution.py:128
  93.4 8.4 %collective-permute-start.12 = (bf16[4,1,64,128]{3,2,1,0:T(8,128)(2,1)S(1)}, bf16[4,1,64,128]{3,2,1,0:T(8,128)(2,1)S(1)}, u32[]{:S(2)}, u32[]{:S(2)}) collective-permute-start(bf16[4,1,64,128]{3,2,1,0:T(8,128)(2,1)S(1)} %get-tuple-element.28), channel_id=1, source_target_pairs={{2,4},{4,2},{3,5},{5,3},{10,12},{12,10},{11,13},{13,11},{18,20},{2... | collective-permute-start | bytes 196616 | tf_op jit(solution)/shard_map/ppermute | solution.py:76
  94.2 7.6 %collective-permute-start.13 = (bf16[4,1,64,128]{3,2,1,0:T(8,128)(2,1)S(1)}, bf16[4,1,64,128]{3,2,1,0:T(8,128)(2,1)S(1)}, u32[]{:S(2)}, u32[]{:S(2)}) collective-permute-start(bf16[4,1,64,128]{3,2,1,0:T(8,128)(2,1)S(1)} %get-tuple-element.27), channel_id=1, source_target_pairs={{0,2},{2,0},{4,6},{6,4},{1,3},{3,1},{5,7},{7,5},{8,10},{10,8},{12,... | collective-permute-start | bytes 196616 | tf_op jit(solution)/shard_map/ppermute | solution.py:72
  97.1 7.1 %collective-permute-start.10 = (bf16[1,8,64,128]{3,2,1,0:T(8,128)(2,1)S(1)}, bf16[1,8,64,128]{3,2,1,0:T(8,128)(2,1)S(1)}, u32[]{:S(2)}, u32[]{:S(2)}) collective-permute-start(bf16[1,8,64,128]{3,2,1,0:T(8,128)(2,1)S(1)} %get-tuple-element.30), channel_id=1, source_target_pairs={{8,16},{16,8},{24,32},{32,24},{40,48},{48,40},{56,64},{64,56},{72,... | collective-permute-start | bytes 393224 | tf_op jit(solution)/shard_map/ppermute | solution.py:76
  101.6 2.6 %collective-permute-start.11 = (bf16[1,8,64,128]{3,2,1,0:T(8,128)(2,1)S(1)}, bf16[1,8,64,128]{3,2,1,0:T(8,128)(2,1)S(1)}, u32[]{:S(2)}, u32[]{:S(2)}) collective-permute-start(bf16[1,8,64,128]{3,2,1,0:T(8,128)(2,1)S(1)} %get-tuple-element.29), channel_id=1, source_target_pairs={{0,8},{8,0},{16,24},{24,16},{32,40},{40,32},{48,56},{56,48},{64,72... | collective-permute-start | bytes 393224 | tf_op jit(solution)/shard_map/ppermute | solution.py:72
  104.3 0.9 copy-start.26
  104.9 4.1 %copy-start.9 = (bf16[6,4,8,64,128]{4,3,2,1,0:T(8,128)(2,1)}, bf16[6,4,8,64,128]{4,3,2,1,0:T(8,128)(2,1)S(1)}, u32[]{:S(2)}) copy-start(bf16[6,4,8,64,128]{4,3,2,1,0:T(8,128)(2,1)S(1)} %fusion.66) | copy-start | bytes 9437188
  105.2 3.9 %copy-start.17 = (bf16[6,4,8,64,128]{4,3,2,1,0:T(8,128)(2,1)S(1)}, bf16[6,4,8,64,128]{4,3,2,1,0:T(8,128)(2,1)}, u32[]{:S(2)}) copy-start(bf16[6,4,8,64,128]{4,3,2,1,0:T(8,128)(2,1)} %copy-done.16) | copy-start | bytes 9437188
  109.1 28.1 %copy-start.24 = (f32[6,128,128]{2,1,0:T(8,128)S(1)}, f32[6,128,128]{2,1,0:T(8,128)}, u32[]{:S(2)}) copy-start(f32[6,128,128]{2,1,0:T(8,128)} %get-tuple-element.41) | copy-start | bytes 1179652
  115.4 39.3 %all-to-all-start = ((f32[256,1,384]{2,1,0:T(1,128)}), f32[256,1,384]{2,1,0:T(1,128)}, u32[]{:S(2)}, u32[]{:S(2)}) async-start(f32[256,1,384]{2,1,0:T(1,128)} %bitcast.75), calls=%async_computation | async-start | bytes 786432 | tf_op jit(solution)/shard_map/all_to_all | solution.py:190
  138.0 25.4 %copy-start.2 = (bf16[6,4,8,64,128]{4,3,2,1,0:T(8,128)(2,1)S(1)}, bf16[6,4,8,64,128]{4,3,2,1,0:T(8,128)(2,1)}, u32[]{:S(2)}) copy-start(bf16[6,4,8,64,128]{4,3,2,1,0:T(8,128)(2,1)} %param.8) | copy-start | bytes 9437188
  157.7 24.2 %all-to-all-start.1 = ((f32[256,1,384]{2,1,0:T(1,128)}), f32[256,1,384]{2,1,0:T(1,128)S(1)}, u32[]{:S(2)}, u32[]{:S(2)}) async-start(f32[256,1,384]{2,1,0:T(1,128)} %broadcast_in_dim.27), calls=%async_computation.1 | async-start | bytes 786432 | tf_op jit(solution)/shard_map/all_to_all | solution.py:193
where the time goes:
time: 184 us; the launch traced here: 183 us
  starting transfers between devices  55.8 us (30%)
  other arithmetic  53.9 us (29%)
  matrix products  32.9 us (18%)
  waiting for transfers between devices  25 us (14%)
  local copies, waits for them, and re-layouts  13.4 us (7%)
    all_to_all x1, starting transfers between devices, all_sum(): lax.all_to_all(rows, axes, 0, 0, tiled=True)  21.8 us
    ppermute x6, starting transfers between devices, trade(): lax.ppermute(jnp.where(odd, high_face, low_face), axis, [(i, i + 1 if i %...  15 us
    ppermute x9, starting transfers between devices, trade(): lax.ppermute(jnp.where(odd, low_face, high_face), axis, [(i, i ^ 1) for i...  13.2 us
    dot_general x2, matrix products, local_adjoint(): jnp.einsum('dxyzl,dkl->dxyzk', grad_out, weights_b, preferred_element_typ...  12.8 us
    dot_general x2, matrix products, local_adjoint(): jnp.einsum('dxyzk,dxyzl->dkl', hidden_b, grad_out, preferred_element_type...  11.9 us
    sub x1, other arithmetic, belief_adjoint(): cotangent - jnp.sum(cotangent * belief, axis=-1, keepdims=True)  11.2 us
    all_to_all x1, waiting for transfers between devices, all_sum(): lax.all_to_all(spread_out, axes, 0, 0, tiled=True).reshape(value.shape)  10.9 us
    all_to_all x1, waiting for transfers between devices, all_sum(): lax.all_to_all(rows, axes, 0, 0, tiled=True)  9.37 us
  transfers between devices with their start and end apart: 17, of which 4 were waited for; matrix products, arithmetic and copies ran while one was open for 19% of the time, Pallas kernels for 0%

commit v1 on v0

--- a/solution.py
+++ b/solution.py
@@ -165,7 +165,8 @@
 
 
 def adjoint_terms(grad_hidden, potential, messages, whole):
-    ratios = [grad_hidden[OPPOSE[index]] / messages[index] for index in range(6)]
+    inverses = [1.0 / messages[index] for index in range(6)]
+    ratios = [grad_hidden[OPPOSE[index]] * inverses[index] for index in range(6)]
     total = ratios[0]
     for index in range(1, 6):
         total = total + ratios[index]
@@ -178,7 +179,7 @@
             if index == edge:
                 continue
             partial_sum = ratios[index] if partial_sum is None else partial_sum + ratios[index]
-        grad_messages.append((partial_sum * (scaled / messages[edge])).astype(jnp.bfloat16))
+        grad_messages.append((partial_sum * (scaled * inverses[edge])).astype(jnp.bfloat16))
     return (unary_term, grad_messages)
 
 

time: 184 us -> 184 us (level)
  no operation moved by 1% of the time
where the time goes in v1:
time: 184 us; the launch traced here: 183 us
  starting transfers between devices  55.8 us (30%)
  other arithmetic  53.9 us (29%)
  matrix products  32.9 us (18%)
  waiting for transfers between devices  25 us (14%)
  local copies, waits for them, and re-layouts  13.4 us (7%)
    all_to_all x1, starting transfers between devices, all_sum(): lax.all_to_all(rows, axes, 0, 0, tiled=True)  21.8 us
    ppermute x6, starting transfers between devices, trade(): lax.ppermute(jnp.where(odd, high_face, low_face), axis, [(i, i + 1 if i %...  15 us
    ppermute x9, starting transfers between devices, trade(): lax.ppermute(jnp.where(odd, low_face, high_face), axis, [(i, i ^ 1) for i...  13.2 us
    dot_general x2, matrix products, local_adjoint(): jnp.einsum('dxyzl,dkl->dxyzk', grad_out, weights_b, preferred_element_typ...  12.8 us
    dot_general x2, matrix products, local_adjoint(): jnp.einsum('dxyzk,dxyzl->dkl', hidden_b, grad_out, preferred_element_type...  11.9 us
    sub x1, other arithmetic, belief_adjoint(): cotangent - jnp.sum(cotangent * belief, axis=-1, keepdims=True)  11.2 us
    all_to_all x1, waiting for transfers between devices, all_sum(): lax.all_to_all(spread_out, axes, 0, 0, tiled=True).reshape(value.shape)  10.9 us
    all_to_all x1, waiting for transfers between devices, all_sum(): lax.all_to_all(rows, axes, 0, 0, tiled=True)  9.37 us
  transfers between devices with their start and end apart: 17, of which 4 were waited for; matrix products, arithmetic and copies ran while one was open for 19% of the time, Pallas kernels for 0%

profile of v1, /device:TPU:1, one launch (start us, length us, event | category | flops | bytes accessed | tf_op | source)
XLA Modules:
  0.0 182.7 jit_solution(13829730133757320250)
XLA Ops:
  0.7 4.7 %bitcast_dynamic-update-slice_fusion.5 = (bf16[6,4,8,64,128]{4,3,2,1,0:T(8,128)(2,1)S(1)}, f32[4,8,64,128]{3,2,1,0:T(8,128)S(1)}, bf16[6,4,8,64,128]{4,3,2,1,0:T(8,128)(2,1)S(1)}, f32[4,8,64,128]{3,2,1,0:T(8,128)S(1)}) fusion(bf16[6,4,8,64,128]{4,3,2,1,0:T(8,128)(2,1)} %param.7, bf16[4,8,64,128]{3,2,1,0:T(8,128)(2,1)} %param.5, ...), kind=kLoop, calls=%fused_computation.167 | loop fusion | flops 7602174 | bytes 9961472
  6.3 1.2 copy-done.5
  8.4 0.3 copy-done.27
  8.7 0.8 fusion.97
  9.5 0.4 bitcast_dynamic-update-slice_fusion
  10.0 1.6 copy-done.16
  11.6 1.9 %fusion.98 = (f32[6,4,8,64]{3,2,1,0:T(8,128)S(1)}, f32[6,4,8,64,128]{4,3,2,1,0:T(8,128)S(1)}) fusion(bf16[6,4,8,64,128]{4,3,2,1,0:T(8,128)(2,1)S(1)} %get-tuple-element.69, bf16[6,128,128]{2,1,0:T(8,128)(2,1)S(1)} %get-tuple-element.42), kind=kOutput, calls=%fused_computation.232 | convolution fusion | flops 404213760 | bytes 9682944 | tf_op jit(solution)/shard_map/dxyzk,dkl->dxyzl/dot_general | solution.py:60
  13.5 2.0 %multiply_convert_fusion = bf16[6,4,8,64,128]{4,3,2,1,0:T(8,128)(2,1)S(1)} fusion(f32[6,4,8,64,128]{4,3,2,1,0:T(8,128)S(1)} %get-tuple-element.64, f32[6,4,8,64]{3,2,1,0:T(8,128)S(1)} %broadcast_divide_fusion.1), kind=kLoop, calls=%fused_computation.11 | loop fusion | flops 3145728 | bytes 9486336 | tf_op jit(solution)/shard_map/convert.29
  15.5 0.6 copy-done.3
  16.1 1.1 slice_bitcast_fusion.13
  17.3 0.8 copy-done.11
  18.1 2.6 %collective-permute-start.4 = (bf16[4,8,1,128]{3,2,1,0:T(2,128)(2,1)S(1)}, bf16[4,8,1,128]{3,2,1,0:T(2,128)(2,1)S(1)}, u32[]{:S(2)}, u32[]{:S(2)}) collective-permute-start(bf16[4,8,1,128]{3,2,1,0:T(2,128)(2,1)S(1)} %broadcast_select_fusion.27), channel_id=1, source_target_pairs={{0,1},{1,0},{2,3},{3,2},{4,5},{5,4},{6,7},{7,6},{8,9},{9,8},{10,11... | collective-permute-start | bytes 24584 | tf_op jit(solution)/shard_map/ppermute | solution.py:72
  20.6 1.7 select_bitcast_fusion.1
  22.3 1.0 collective-permute-start
  23.3 3.0 %collective-permute-start.1 = (bf16[1,8,64,128]{3,2,1,0:T(8,128)(2,1)}, bf16[1,8,64,128]{3,2,1,0:T(8,128)(2,1)}, u32[]{:S(2)}, u32[]{:S(2)}) collective-permute-start(bf16[1,8,64,128]{3,2,1,0:T(8,128)(2,1)} %get-tuple-element.26), channel_id=1, source_target_pairs={{8,16},{16,8},{24,32},{32,24},{40,48},{48,40},{56,64},{64,56},{72,... | collective-permute-start | bytes 393224 | tf_op jit(solution)/shard_map/ppermute | solution.py:76
  26.3 1.5 broadcast_select_fusion.17
  27.8 1.3 collective-permute-start.2
  29.1 1.3 collective-permute-start.3
  30.4 1.9 %slice_bitcast_fusion.17 = (bf16[3,8,64,128]{3,2,1,0:T(8,128)(2,1)}, bf16[3,8,64,128]{3,2,1,0:T(8,128)(2,1)S(1)}) fusion(bf16[6,4,8,64,128]{4,3,2,1,0:T(8,128)(2,1)} %copy-done.11), kind=kLoop, calls=%fused_computation.177 | loop fusion | bytes 1572864 | tf_op jit(solution)/shard_map/slice | solution.py:104
  32.3 6.3 %fusion.99 = (f32[6,4,8,64]{3,2,1,0:T(8,128)S(1)}, f32[6,4,8,64,128]{4,3,2,1,0:T(8,128)}) fusion(bf16[6,4,8,64,128]{4,3,2,1,0:T(8,128)(2,1)} %copy-done.16, bf16[6,128,128]{2,1,0:T(8,128)(2,1)S(1)} %get-tuple-element.42), kind=kOutput, calls=%fused_computation.233 | convolution fusion | flops 404213760 | bytes 9682944 | tf_op jit(solution)/shard_map/dxyzk,dkl->dxyzl/dot_general | solution.py:60
  38.6 0.7 broadcast_divide_fusion
  39.4 1.2 slice.286
  40.7 1.1 slice.287
  41.9 1.0 select_select_fusion.3
  42.9 1.0 select_select_fusion.1
  43.9 1.9 %fusion.90 = (f32[4,8,64]{2,1,0:T(8,128)S(1)}, f32[4,8,64,128]{3,2,1,0:T(8,128)S(1)}) fusion(bf16[4,8,64,128]{3,2,1,0:T(8,128)(2,1)} %param.5, bf16[4,8,1,128]{3,2,1,0:T(2,128)(2,1)S(1)} %get-tuple-element.62, bf16[4,8,63,128]{3,2,1,0:T(8,128)(2,1)S(1)} %slice.293, bf16[4,8,63,128]{3,2,1,0:T(8,128)(2,1)S(1)} %bitcast.360, ...), kind=kLoop, calls=%fused_computation.230 | loop fusion | flops 8386560 | bytes 4726784 | tf_op jit(solution)/shard_map/reduce_sum | solution.py:143
  45.8 11.2 %fusion.35 = (bf16[4,8,64,128]{3,2,1,0:T(8,128)(2,1)S(1)}, f32[4,8,64,128]{3,2,1,0:T(8,128)S(1)}, f32[4,8,64,128]{3,2,1,0:T(8,128)}) fusion(bf16[4,1,64,128]{3,2,1,0:T(8,128)(2,1)S(1)} %get-tuple-element.54, bf16[4,7,64,128]{3,2,1,0:T(8,128)(2,1)S(1)} %slice.287, bf16[4,7,64,128]{3,2,1,0:T(8,128)(2,1)S(1)} %slice.286, ...), kind=kOutput, calls=%fused_computation.73 | output fusion | flops 10225791 | bytes 7880704 | tf_op jit(solution)/shard_map/sub | solution.py:146
  57.0 0.8 multiply_convert_fusion.7
  57.8 0.6 multiply_convert_fusion.9
  58.5 0.7 fusion.31
  59.1 0.7 fusion.33
  60.3 0.8 collective-permute-start.7
  61.1 4.6 %collective-permute-start.8 = (bf16[4,1,64,128]{3,2,1,0:T(8,128)(2,1)S(1)}, bf16[4,1,64,128]{3,2,1,0:T(8,128)(2,1)S(1)}, u32[]{:S(2)}, u32[]{:S(2)}) collective-permute-start(bf16[4,1,64,128]{3,2,1,0:T(8,128)(2,1)S(1)} %get-tuple-element.33), channel_id=1, source_target_pairs={{0,2},{2,0},{4,6},{6,4},{1,3},{3,1},{5,7},{7,5},{8,10},{10,8},{12,... | collective-permute-start | bytes 196616 | tf_op jit(solution)/shard_map/ppermute | solution.py:72
  65.7 4.6 %collective-permute-start.5 = (bf16[1,8,64,128]{3,2,1,0:T(8,128)(2,1)S(1)}, bf16[1,8,64,128]{3,2,1,0:T(8,128)(2,1)S(1)}, u32[]{:S(2)}, u32[]{:S(2)}) collective-permute-start(bf16[1,8,64,128]{3,2,1,0:T(8,128)(2,1)S(1)} %get-tuple-element.36), channel_id=1, source_target_pairs={{8,16},{16,8},{24,32},{32,24},{40,48},{48,40},{56,64},{64,56},{72,... | collective-permute-start | bytes 393224 | tf_op jit(solution)/shard_map/ppermute | solution.py:76
  70.4 0.3 collective-permute-start.6
  70.8 2.2 %collective-permute-done.5 = bf16[1,8,64,128]{3,2,1,0:T(8,128)(2,1)S(1)} collective-permute-done((bf16[1,8,64,128]{3,2,1,0:T(8,128)(2,1)S(1)}, bf16[1,8,64,128]{3,2,1,0:T(8,128)(2,1)S(1)}, u32[]{:S(2)}, u32[]{:S(2)}) %collective-permute-start.5) | collective-permute-done | bytes 131104 | tf_op jit(solution)/shard_map/ppermute | solution.py:76
  73.4 0.2 fusion.72
  73.7 3.8 %fusion.1 = f32[6,4,8,64]{3,2,1,0:T(8,128)S(1)} fusion(bf16[6,4,8,64,128]{4,3,2,1,0:T(8,128)(2,1)S(1)} %fusion.72, f32[6,4,8,64,128]{4,3,2,1,0:T(8,128)S(1)} %bitcast.357, f32[6,4,8,64]{3,2,1,0:T(8,128)S(1)} %broadcast_divide_fusion.1), kind=kLoop, calls=%fused_computation.5 | loop fusion | flops 6279168 | bytes 9535488 | tf_op jit(solution)/shard_map/reduce_sum | solution.py:156
  77.5 5.7 %fusion.15 = f32[6,128,128]{2,1,0:T(8,128)S(1)} fusion(bf16[6,4,8,64,128]{4,3,2,1,0:T(8,128)(2,1)S(1)} %copy-done.19, bf16[6,4,8,64,128]{4,3,2,1,0:T(8,128)(2,1)S(1)} %fusion.72, f32[6,4,8,64]{3,2,1,0:T(8,128)S(1)} %broadcast_multiply_fusion.1, f32[6,4,8,64]{3,2,1,0:T(8,128)S(1)} %broadcast_divide_fusion.1), kind=kOutput, calls=%fused_computation.65 | convolution fusion | flops 408944640 | bytes 6782976 | tf_op jit(solution)/shard_map/dxyzk,dxyzl->dkl/dot_general | solution.py:158
  83.2 5.5 %fusion.84 = f32[6,4,8,64,128]{4,3,2,1,0:T(8,128)S(1)} fusion(bf16[6,128,128]{2,1,0:T(8,128)(2,1)S(1)} %copy-done.15, bf16[6,4,8,64,128]{4,3,2,1,0:T(8,128)(2,1)S(1)} %fusion.72, f32[6,4,8,64]{3,2,1,0:T(8,128)S(1)} %broadcast_multiply_fusion.1, f32[6,4,8,64]{3,2,1,0:T(8,128)S(1)} %broadcast_divide_fusion.1), kind=kOutput, calls=%fused_computation.182 | convolution fusion | flops 408944640 | bytes 9732096 | tf_op jit(solution)/shard_map/dxyzl,dkl->dxyzk/dot_general | solution.py:161
  88.8 1.1 multiply_convert_fusion.2
  89.9 0.5 multiply_convert_fusion.1
  90.4 0.4 collective-permute-start.14
  90.8 1.0 multiply_convert_fusion.6
  91.8 1.2 multiply_convert_fusion.3
  93.4 0.8 collective-permute-start.12
  94.2 2.9 %collective-permute-start.13 = (bf16[4,1,64,128]{3,2,1,0:T(8,128)(2,1)S(1)}, bf16[4,1,64,128]{3,2,1,0:T(8,128)(2,1)S(1)}, u32[]{:S(2)}, u32[]{:S(2)}) collective-permute-start(bf16[4,1,64,128]{3,2,1,0:T(8,128)(2,1)S(1)} %get-tuple-element.27), channel_id=1, source_target_pairs={{0,2},{2,0},{4,6},{6,4},{1,3},{3,1},{5,7},{7,5},{8,10},{10,8},{12,... | collective-permute-start | bytes 196616 | tf_op jit(solution)/shard_map/ppermute | solution.py:72
  97.1 4.5 %collective-permute-start.10 = (bf16[1,8,64,128]{3,2,1,0:T(8,128)(2,1)S(1)}, bf16[1,8,64,128]{3,2,1,0:T(8,128)(2,1)S(1)}, u32[]{:S(2)}, u32[]{:S(2)}) collective-permute-start(bf16[1,8,64,128]{3,2,1,0:T(8,128)(2,1)S(1)} %get-tuple-element.30), channel_id=1, source_target_pairs={{8,16},{16,8},{24,32},{32,24},{40,48},{48,40},{56,64},{64,56},{72,... | collective-permute-start | bytes 393224 | tf_op jit(solution)/shard_map/ppermute | solution.py:76
  101.8 2.4 %collective-permute-done.10 = bf16[1,8,64,128]{3,2,1,0:T(8,128)(2,1)S(1)} collective-permute-done((bf16[1,8,64,128]{3,2,1,0:T(8,128)(2,1)S(1)}, bf16[1,8,64,128]{3,2,1,0:T(8,128)(2,1)S(1)}, u32[]{:S(2)}, u32[]{:S(2)}) %collective-permute-start.10) | collective-permute-done | bytes 131104 | tf_op jit(solution)/shard_map/ppermute | solution.py:76
  104.7 0.2 fusion.78
  105.0 0.2 copy-done.26
  105.2 3.8 %fusion.4 = f32[6,4,8,64]{3,2,1,0:T(8,128)S(1)} fusion(bf16[6,4,8,64,128]{4,3,2,1,0:T(8,128)(2,1)S(1)} %fusion.78, f32[6,4,8,64,128]{4,3,2,1,0:T(8,128)S(1)} %bitcast.359, f32[6,4,8,64]{3,2,1,0:T(8,128)S(1)} %copy-done.26), kind=kLoop, calls=%fused_computation.8 | loop fusion | flops 6279168 | bytes 9535488 | tf_op jit(solution)/shard_map/reduce_sum | solution.py:156
  109.1 6.3 %fusion.25 = f32[6,128,128]{2,1,0:T(8,128)} fusion(f32[6,128,128]{2,1,0:T(8,128)S(1)} %fusion.15, bf16[6,4,8,64,128]{4,3,2,1,0:T(8,128)(2,1)S(1)} %copy-done.17, bf16[6,4,8,64,128]{4,3,2,1,0:T(8,128)(2,1)S(1)} %fusion.78, f32[6,4,8,64]{3,2,1,0:T(8,128)S(1)} %broadcast_multiply_fusion, f32[6,4,8,64]{3,2,1,0:T(8,128)S(1)} %copy-done.26), kind=kOutput, calls=%fused_computation.67 | convolution fusion | flops 409042944 | bytes 7176192 | tf_op jit(solution)/shard_map/dxyzk,dxyzl->dkl/dot_general | solution.py:158
  115.4 21.8 %all-to-all-start = ((f32[256,1,384]{2,1,0:T(1,128)}), f32[256,1,384]{2,1,0:T(1,128)}, u32[]{:S(2)}, u32[]{:S(2)}) async-start(f32[256,1,384]{2,1,0:T(1,128)} %bitcast.75), calls=%async_computation | async-start | bytes 786432 | tf_op jit(solution)/shard_map/all_to_all | solution.py:191
  137.2 0.8 reshape.80
  138.0 7.3 %fusion.80 = f32[6,4,8,64,128]{4,3,2,1,0:T(8,128)} fusion(bf16[6,128,128]{2,1,0:T(8,128)(2,1)S(1)} %copy-done.15, bf16[6,4,8,64,128]{4,3,2,1,0:T(8,128)(2,1)} %copy-done.9, f32[6,4,8,64]{3,2,1,0:T(8,128)S(1)} %broadcast_multiply_fusion, f32[6,4,8,64]{3,2,1,0:T(8,128)S(1)} %copy-done.26), kind=kOutput, calls=%fused_computation.178 | convolution fusion | flops 408944640 | bytes 9732096 | tf_op jit(solution)/shard_map/dxyzl,dkl->dxyzk/dot_general | solution.py:161
  145.3 9.4 %all-to-all-done = f32[256,1,384]{2,1,0:T(1,128)} async-done(((f32[256,1,384]{2,1,0:T(1,128)}), f32[256,1,384]{2,1,0:T(1,128)}, u32[]{:S(2)}, u32[]{:S(2)}) %all-to-all-start) | async-done | bytes 393248 | tf_op jit(solution)/shard_map/all_to_all | solution.py:191
  154.7 1.3 reduce_sum.69
  156.0 0.7 multiply_reduce_fusion
  156.7 1.0 broadcast_in_dim.27
  157.7 5.8 %all-to-all-start.1 = ((f32[256,1,384]{2,1,0:T(1,128)}), f32[256,1,384]{2,1,0:T(1,128)S(1)}, u32[]{:S(2)}, u32[]{:S(2)}) async-start(f32[256,1,384]{2,1,0:T(1,128)} %broadcast_in_dim.27), calls=%async_computation.1 | async-start | bytes 786432 | tf_op jit(solution)/shard_map/all_to_all | solution.py:194
  163.5 7.6 %fusion.50 = f32[4,8,64,128]{3,2,1,0:T(8,128)} fusion(f32[6,4,8,64,128]{4,3,2,1,0:T(8,128)} %fusion.80, f32[4,8,64,128]{3,2,1,0:T(8,128)} %copy-done.6, f32[4,8,64,128]{3,2,1,0:T(8,128)} %get-tuple-element.65, bf16[4,8,64,128]{3,2,1,0:T(8,128)(2,1)} %param.5, f32[4,8,64,128]{3,2,1,0:T(8,128)} %copy-done.8, f32[4,8,64,128]{3,2,1,0:T(8,128)} %copy-done.12, ...), kind=kLoop, calls=%fused_computation.88 | loop fusion | flops 12320768 | bytes 19922944 | tf_op jit(solution)/shard_map/mul | solution.py:233
  171.0 10.9 %all-to-all-done.1 = f32[256,1,384]{2,1,0:T(1,128)S(1)} async-done(((f32[256,1,384]{2,1,0:T(1,128)}), f32[256,1,384]{2,1,0:T(1,128)S(1)}, u32[]{:S(2)}, u32[]{:S(2)}) %all-to-all-start.1) | async-done | bytes 393248 | tf_op jit(solution)/shard_map/all_to_all | solution.py:194
  181.9 0.7 copy.56
  (125 shorter events, 3.9 us)
Async XLA Ops:
  0.6 4.7 %copy-start = (bf16[6,4,8,64,128]{4,3,2,1,0:T(8,128)(2,1)S(1)}, bf16[6,4,8,64,128]{4,3,2,1,0:T(8,128)(2,1)}, u32[]{:S(2)}) copy-start(bf16[6,4,8,64,128]{4,3,2,1,0:T(8,128)(2,1)} %param.8) | copy-start | bytes 9437188
  5.6 1.9 %copy-start.5 = (bf16[6,4,8,64,128]{4,3,2,1,0:T(8,128)(2,1)S(1)}, bf16[6,4,8,64,128]{4,3,2,1,0:T(8,128)(2,1)}, u32[]{:S(2)}) copy-start(bf16[6,4,8,64,128]{4,3,2,1,0:T(8,128)(2,1)} %param.7) | copy-start | bytes 9437188
  7.7 1.0 copy-start.27
  9.5 22.8 %copy-start.14 = (bf16[6,128,128]{2,1,0:T(8,128)(2,1)}, bf16[6,128,128]{2,1,0:T(8,128)(2,1)S(1)}, u32[]{:S(2)}) copy-start(bf16[6,128,128]{2,1,0:T(8,128)(2,1)S(1)} %get-tuple-element.42) | copy-start | bytes 589828
  10.0 1.6 copy-start.16
  10.0 3.5 %copy-start.18 = (bf16[6,4,8,64,128]{4,3,2,1,0:T(8,128)(2,1)}, bf16[6,4,8,64,128]{4,3,2,1,0:T(8,128)(2,1)S(1)}, u32[]{:S(2)}) copy-start(bf16[6,4,8,64,128]{4,3,2,1,0:T(8,128)(2,1)S(1)} %get-tuple-element.69) | copy-start | bytes 9437188
  13.5 2.6 %copy-start.3 = (f32[6,4,8,64,128]{4,3,2,1,0:T(8,128)}, f32[6,4,8,64,128]{4,3,2,1,0:T(8,128)S(1)}, u32[]{:S(2)}) copy-start(f32[6,4,8,64,128]{4,3,2,1,0:T(8,128)S(1)} %get-tuple-element.64) | copy-start | bytes 18874372
  16.1 1.9 %copy-start.11 = (bf16[6,4,8,64,128]{4,3,2,1,0:T(8,128)(2,1)}, bf16[6,4,8,64,128]{4,3,2,1,0:T(8,128)(2,1)S(1)}, u32[]{:S(2)}) copy-start(bf16[6,4,8,64,128]{4,3,2,1,0:T(8,128)(2,1)S(1)} %multiply_convert_fusion) | copy-start | bytes 9437188
  18.0 11.1 %copy-start.22 = (bf16[4,8,64,128]{3,2,1,0:T(8,128)(2,1)}, bf16[4,8,64,128]{3,2,1,0:T(8,128)(2,1)S(1)}, u32[]{:S(2)}) copy-start(bf16[4,8,64,128]{3,2,1,0:T(8,128)(2,1)S(1)} %get-tuple-element.22) | copy-start | bytes 1572868
  18.1 23.7 %collective-permute-start.4 = (bf16[4,8,1,128]{3,2,1,0:T(2,128)(2,1)S(1)}, bf16[4,8,1,128]{3,2,1,0:T(2,128)(2,1)S(1)}, u32[]{:S(2)}, u32[]{:S(2)}) collective-permute-start(bf16[4,8,1,128]{3,2,1,0:T(2,128)(2,1)S(1)} %broadcast_select_fusion.27), channel_id=1, source_target_pairs={{0,1},{1,0},{2,3},{3,2},{4,5},{5,4},{6,7},{7,6},{8,9},{9,8},{10,11... | collective-permute-start | bytes 24584 | tf_op jit(solution)/shard_map/ppermute | solution.py:72
  22.3 20.6 %collective-permute-start = (bf16[1,8,64,128]{3,2,1,0:T(8,128)(2,1)}, bf16[1,8,64,128]{3,2,1,0:T(8,128)(2,1)}, u32[]{:S(2)}, u32[]{:S(2)}) collective-permute-start(bf16[1,8,64,128]{3,2,1,0:T(8,128)(2,1)} %get-tuple-element.25), channel_id=1, source_target_pairs={{0,8},{8,0},{16,24},{24,16},{32,40},{40,32},{48,56},{56,48},{64,72... | collective-permute-start | bytes 393224 | tf_op jit(solution)/shard_map/ppermute | solution.py:72
  23.3 19.6 %collective-permute-start.1 = (bf16[1,8,64,128]{3,2,1,0:T(8,128)(2,1)}, bf16[1,8,64,128]{3,2,1,0:T(8,128)(2,1)}, u32[]{:S(2)}, u32[]{:S(2)}) collective-permute-start(bf16[1,8,64,128]{3,2,1,0:T(8,128)(2,1)} %get-tuple-element.26), channel_id=1, source_target_pairs={{8,16},{16,8},{24,32},{32,24},{40,48},{48,40},{56,64},{64,56},{72,... | collective-permute-start | bytes 393224 | tf_op jit(solution)/shard_map/ppermute | solution.py:76
  27.8 14.0 %collective-permute-start.2 = (bf16[4,1,64,128]{3,2,1,0:T(8,128)(2,1)}, bf16[4,1,64,128]{3,2,1,0:T(8,128)(2,1)}, u32[]{:S(2)}, u32[]{:S(2)}) collective-permute-start(bf16[4,1,64,128]{3,2,1,0:T(8,128)(2,1)} %get-tuple-element.37), channel_id=1, source_target_pairs={{0,2},{2,0},{4,6},{6,4},{1,3},{3,1},{5,7},{7,5},{8,10},{10,8},{12,... | collective-permute-start | bytes 196616 | tf_op jit(solution)/shard_map/ppermute | solution.py:72
  29.1 12.7 %collective-permute-start.3 = (bf16[4,1,64,128]{3,2,1,0:T(8,128)(2,1)}, bf16[4,1,64,128]{3,2,1,0:T(8,128)(2,1)}, u32[]{:S(2)}, u32[]{:S(2)}) collective-permute-start(bf16[4,1,64,128]{3,2,1,0:T(8,128)(2,1)} %get-tuple-element.38), channel_id=1, source_target_pairs={{2,4},{4,2},{3,5},{5,3},{10,12},{12,10},{11,13},{13,11},{18,20},{2... | collective-permute-start | bytes 196616 | tf_op jit(solution)/shard_map/ppermute | solution.py:76
  39.4 19.7 %copy-start.4 = (bf16[4,8,63,128]{3,2,1,0:T(8,128)(2,1)}, bf16[4,8,63,128]{3,2,1,0:T(8,128)(2,1)S(1)}, u32[]{:S(2)}) copy-start(bf16[4,8,63,128]{3,2,1,0:T(8,128)(2,1)S(1)} %slice.293) | copy-start | bytes 1548292
  41.7 4.1 %copy-start.10 = (bf16[3,8,64,128]{3,2,1,0:T(8,128)(2,1)S(1)}, bf16[3,8,64,128]{3,2,1,0:T(8,128)(2,1)}, u32[]{:S(2)}) copy-start(bf16[3,8,64,128]{3,2,1,0:T(8,128)(2,1)} %get-tuple-element.23) | copy-start | bytes 1179652
  41.8 4.1 %copy-start.13 = (bf16[4,8,64,128]{3,2,1,0:T(8,128)(2,1)S(1)}, bf16[4,8,64,128]{3,2,1,0:T(8,128)(2,1)}, u32[]{:S(2)}) copy-start(bf16[4,8,64,128]{3,2,1,0:T(8,128)(2,1)} %param.5) | copy-start | bytes 1572868
  41.8 4.1 %copy-start.25 = (f32[4,8,64,128]{3,2,1,0:T(8,128)S(1)}, f32[4,8,64,128]{3,2,1,0:T(8,128)}, u32[]{:S(2)}) copy-start(f32[4,8,64,128]{3,2,1,0:T(8,128)} %param.9) | copy-start | bytes 3145732
  45.8 11.3 %copy-start.8 = (f32[4,8,64,128]{3,2,1,0:T(8,128)}, f32[4,8,64,128]{3,2,1,0:T(8,128)S(1)}, u32[]{:S(2)}) copy-start(f32[4,8,64,128]{3,2,1,0:T(8,128)S(1)} %get-tuple-element.13) | copy-start | bytes 3145732
  58.4 1.6 copy-start.23
  59.1 0.9 copy-start.21
  59.1 14.5 %slice-start = ((s8[6291456]{0:T(1024)(128)(4,1)}), s8[4194304]{0:T(1024)(128)(4,1)S(1)}, s32[]{:S(2)}) async-start(s8[6291456]{0:T(1024)(128)(4,1)} %bitcast.356), calls=%async_computation.2 | async-start | bytes 8388608
  59.8 10.8 %collective-permute-start.9 = (bf16[4,8,1,128]{3,2,1,0:T(2,128)(2,1)S(1)}, bf16[4,8,1,128]{3,2,1,0:T(2,128)(2,1)S(1)}, u32[]{:S(2)}, u32[]{:S(2)}) collective-permute-start(bf16[4,8,1,128]{3,2,1,0:T(2,128)(2,1)S(1)} %broadcast_select_fusion.24), channel_id=1, source_target_pairs={{0,1},{1,0},{2,3},{3,2},{4,5},{5,4},{6,7},{7,6},{8,9},{9,8},{10,11... | collective-permute-start | bytes 24584 | tf_op jit(solution)/shard_map/ppermute | solution.py:72
  60.0 13.1 %slice-start.6 = ((bf16[4,8,64,128]{3,2,1,0:T(8,128)(2,1)}), bf16[4,7,64,128]{3,2,1,0:T(8,128)(2,1)S(1)}, s32[]{:S(2)}) async-start(bf16[4,8,64,128]{3,2,1,0:T(8,128)(2,1)} %copy-done.23), calls=%async_computation.8 | async-start | bytes 917504 | tf_op jit(solution)/shard_map/slice | solution.py:128
  60.1 13.0 %slice-start.5 = ((bf16[4,8,64,128]{3,2,1,0:T(8,128)(2,1)}), bf16[3,8,64,128]{3,2,1,0:T(8,128)(2,1)S(1)}, s32[]{:S(2)}) async-start(bf16[4,8,64,128]{3,2,1,0:T(8,128)(2,1)} %copy-done.21), calls=%async_computation.7 | async-start | bytes 786432 | tf_op jit(solution)/shard_map/slice | solution.py:133
  60.1 13.6 %slice-start.1 = ((s8[6291456]{0:T(1024)(128)(4,1)}), s8[2097152]{0:T(1024)(128)(4,1)S(1)}, s32[]{:S(2)}) async-start(s8[6291456]{0:T(1024)(128)(4,1)} %bitcast.356), calls=%async_computation.3 | async-start | bytes 4194304
  60.3 10.4 %collective-permute-start.7 = (bf16[4,1,64,128]{3,2,1,0:T(8,128)(2,1)S(1)}, bf16[4,1,64,128]{3,2,1,0:T(8,128)(2,1)S(1)}, u32[]{:S(2)}, u32[]{:S(2)}) collective-permute-start(bf16[4,1,64,128]{3,2,1,0:T(8,128)(2,1)S(1)} %get-tuple-element.34), channel_id=1, source_target_pairs={{2,4},{4,2},{3,5},{5,3},{10,12},{12,10},{11,13},{13,11},{18,20},{2... | collective-permute-start | bytes 196616 | tf_op jit(solution)/shard_map/ppermute | solution.py:76
  61.1 9.6 %collective-permute-start.8 = (bf16[4,1,64,128]{3,2,1,0:T(8,128)(2,1)S(1)}, bf16[4,1,64,128]{3,2,1,0:T(8,128)(2,1)S(1)}, u32[]{:S(2)}, u32[]{:S(2)}) collective-permute-start(bf16[4,1,64,128]{3,2,1,0:T(8,128)(2,1)S(1)} %get-tuple-element.33), channel_id=1, source_target_pairs={{0,2},{2,0},{4,6},{6,4},{1,3},{3,1},{5,7},{7,5},{8,10},{10,8},{12,... | collective-permute-start | bytes 196616 | tf_op jit(solution)/shard_map/ppermute | solution.py:72
  65.7 7.3 %collective-permute-start.5 = (bf16[1,8,64,128]{3,2,1,0:T(8,128)(2,1)S(1)}, bf16[1,8,64,128]{3,2,1,0:T(8,128)(2,1)S(1)}, u32[]{:S(2)}, u32[]{:S(2)}) collective-permute-start(bf16[1,8,64,128]{3,2,1,0:T(8,128)(2,1)S(1)} %get-tuple-element.36), channel_id=1, source_target_pairs={{8,16},{16,8},{24,32},{32,24},{40,48},{48,40},{56,64},{64,56},{72,... | collective-permute-start | bytes 393224 | tf_op jit(solution)/shard_map/ppermute | solution.py:76
  70.4 2.6 %collective-permute-start.6 = (bf16[1,8,64,128]{3,2,1,0:T(8,128)(2,1)S(1)}, bf16[1,8,64,128]{3,2,1,0:T(8,128)(2,1)S(1)}, u32[]{:S(2)}, u32[]{:S(2)}) collective-permute-start(bf16[1,8,64,128]{3,2,1,0:T(8,128)(2,1)S(1)} %get-tuple-element.35), channel_id=1, source_target_pairs={{0,8},{8,0},{16,24},{24,16},{32,40},{40,32},{48,56},{56,48},{64,72... | collective-permute-start | bytes 393224 | tf_op jit(solution)/shard_map/ppermute | solution.py:72
  73.7 3.8 %copy-start.19 = (bf16[6,4,8,64,128]{4,3,2,1,0:T(8,128)(2,1)S(1)}, bf16[6,4,8,64,128]{4,3,2,1,0:T(8,128)(2,1)}, u32[]{:S(2)}) copy-start(bf16[6,4,8,64,128]{4,3,2,1,0:T(8,128)(2,1)} %copy-done.18) | copy-start | bytes 9437188
  77.5 5.7 %copy-start.15 = (bf16[6,128,128]{2,1,0:T(8,128)(2,1)S(1)}, bf16[6,128,128]{2,1,0:T(8,128)(2,1)}, u32[]{:S(2)}) copy-start(bf16[6,128,128]{2,1,0:T(8,128)(2,1)} %copy-done.14) | copy-start | bytes 589828
  83.2 5.6 %copy-start.1 = (bf16[6,4,8,64,128]{4,3,2,1,0:T(8,128)(2,1)S(1)}, bf16[6,4,8,64,128]{4,3,2,1,0:T(8,128)(2,1)}, u32[]{:S(2)}) copy-start(bf16[6,4,8,64,128]{4,3,2,1,0:T(8,128)(2,1)} %param.8) | copy-start | bytes 9437188
  89.9 1.9 %copy-start.12 = (f32[4,8,64,128]{3,2,1,0:T(8,128)}, f32[4,8,64,128]{3,2,1,0:T(8,128)S(1)}, u32[]{:S(2)}) copy-start(f32[4,8,64,128]{3,2,1,0:T(8,128)S(1)} %get-tuple-element.5) | copy-start | bytes 3145732
  89.9 1.9 %copy-start.6 = (f32[4,8,64,128]{3,2,1,0:T(8,128)}, f32[4,8,64,128]{3,2,1,0:T(8,128)S(1)}, u32[]{:S(2)}) copy-start(f32[4,8,64,128]{3,2,1,0:T(8,128)S(1)} %get-tuple-element.7) | copy-start | bytes 3145732
  90.3 1.5 copy-start.7
  90.4 11.3 %collective-permute-start.14 = (bf16[4,8,1,128]{3,2,1,0:T(2,128)(2,1)S(1)}, bf16[4,8,1,128]{3,2,1,0:T(2,128)(2,1)S(1)}, u32[]{:S(2)}, u32[]{:S(2)}) collective-permute-start(bf16[4,8,1,128]{3,2,1,0:T(2,128)(2,1)S(1)} %broadcast_select_fusion.21), channel_id=1, source_target_pairs={{0,1},{1,0},{2,3},{3,2},{4,5},{5,4},{6,7},{7,6},{8,9},{9,8},{10,11... | collective-permute-start | bytes 24584 | tf_op jit(solution)/shard_map/ppermute | solution.py:72
  91.8 1.3 copy-start.20
  91.8 13.1 %slice-start.2 = ((s8[6291456]{0:T(1024)(128)(4,1)}), s8[2097152]{0:T(1024)(128)(4,1)S(1)}, s32[]{:S(2)}) async-start(s8[6291456]{0:T(1024)(128)(4,1)} %bitcast.358), calls=%async_computation.4 | async-start | bytes 4194304
  93.1 11.9 %slice-start.3 = ((s8[6291456]{0:T(1024)(128)(4,1)}), s8[4194304]{0:T(1024)(128)(4,1)S(1)}, s32[]{:S(2)}) async-start(s8[6291456]{0:T(1024)(128)(4,1)} %bitcast.358), calls=%async_computation.5 | async-start | bytes 8388608
  93.1 11.2 %slice-start.4 = ((bf16[4,8,64,128]{3,2,1,0:T(8,128)(2,1)}), bf16[3,8,64,128]{3,2,1,0:T(8,128)(2,1)S(1)}, s32[]{:S(2)}) async-start(bf16[4,8,64,128]{3,2,1,0:T(8,128)(2,1)} %copy-done.20), calls=%async_computation.6 | async-start | bytes 786432 | tf_op jit(solution)/shard_map/slice | solution.py:128
  93.4 8.4 %collective-permute-start.12 = (bf16[4,1,64,128]{3,2,1,0:T(8,128)(2,1)S(1)}, bf16[4,1,64,128]{3,2,1,0:T(8,128)(2,1)S(1)}, u32[]{:S(2)}, u32[]{:S(2)}) collective-permute-start(bf16[4,1,64,128]{3,2,1,0:T(8,128)(2,1)S(1)} %get-tuple-element.28), channel_id=1, source_target_pairs={{2,4},{4,2},{3,5},{5,3},{10,12},{12,10},{11,13},{13,11},{18,20},{2... | collective-permute-start | bytes 196616 | tf_op jit(solution)/shard_map/ppermute | solution.py:76
  94.2 7.6 %collective-permute-start.13 = (bf16[4,1,64,128]{3,2,1,0:T(8,128)(2,1)S(1)}, bf16[4,1,64,128]{3,2,1,0:T(8,128)(2,1)S(1)}, u32[]{:S(2)}, u32[]{:S(2)}) collective-permute-start(bf16[4,1,64,128]{3,2,1,0:T(8,128)(2,1)S(1)} %get-tuple-element.27), channel_id=1, source_target_pairs={{0,2},{2,0},{4,6},{6,4},{1,3},{3,1},{5,7},{7,5},{8,10},{10,8},{12,... | collective-permute-start | bytes 196616 | tf_op jit(solution)/shard_map/ppermute | solution.py:72
  97.1 7.1 %collective-permute-start.10 = (bf16[1,8,64,128]{3,2,1,0:T(8,128)(2,1)S(1)}, bf16[1,8,64,128]{3,2,1,0:T(8,128)(2,1)S(1)}, u32[]{:S(2)}, u32[]{:S(2)}) collective-permute-start(bf16[1,8,64,128]{3,2,1,0:T(8,128)(2,1)S(1)} %get-tuple-element.30), channel_id=1, source_target_pairs={{8,16},{16,8},{24,32},{32,24},{40,48},{48,40},{56,64},{64,56},{72,... | collective-permute-start | bytes 393224 | tf_op jit(solution)/shard_map/ppermute | solution.py:76
  101.6 2.6 %collective-permute-start.11 = (bf16[1,8,64,128]{3,2,1,0:T(8,128)(2,1)S(1)}, bf16[1,8,64,128]{3,2,1,0:T(8,128)(2,1)S(1)}, u32[]{:S(2)}, u32[]{:S(2)}) collective-permute-start(bf16[1,8,64,128]{3,2,1,0:T(8,128)(2,1)S(1)} %get-tuple-element.29), channel_id=1, source_target_pairs={{0,8},{8,0},{16,24},{24,16},{32,40},{40,32},{48,56},{56,48},{64,72... | collective-permute-start | bytes 393224 | tf_op jit(solution)/shard_map/ppermute | solution.py:72
  104.3 0.9 copy-start.26
  104.9 4.1 %copy-start.9 = (bf16[6,4,8,64,128]{4,3,2,1,0:T(8,128)(2,1)}, bf16[6,4,8,64,128]{4,3,2,1,0:T(8,128)(2,1)S(1)}, u32[]{:S(2)}) copy-start(bf16[6,4,8,64,128]{4,3,2,1,0:T(8,128)(2,1)S(1)} %fusion.78) | copy-start | bytes 9437188
  105.2 3.9 %copy-start.17 = (bf16[6,4,8,64,128]{4,3,2,1,0:T(8,128)(2,1)S(1)}, bf16[6,4,8,64,128]{4,3,2,1,0:T(8,128)(2,1)}, u32[]{:S(2)}) copy-start(bf16[6,4,8,64,128]{4,3,2,1,0:T(8,128)(2,1)} %copy-done.16) | copy-start | bytes 9437188
  109.1 28.1 %copy-start.24 = (f32[6,128,128]{2,1,0:T(8,128)S(1)}, f32[6,128,128]{2,1,0:T(8,128)}, u32[]{:S(2)}) copy-start(f32[6,128,128]{2,1,0:T(8,128)} %get-tuple-element.41) | copy-start | bytes 1179652
  115.4 39.3 %all-to-all-start = ((f32[256,1,384]{2,1,0:T(1,128)}), f32[256,1,384]{2,1,0:T(1,128)}, u32[]{:S(2)}, u32[]{:S(2)}) async-start(f32[256,1,384]{2,1,0:T(1,128)} %bitcast.75), calls=%async_computation | async-start | bytes 786432 | tf_op jit(solution)/shard_map/all_to_all | solution.py:191
  138.0 25.4 %copy-start.2 = (bf16[6,4,8,64,128]{4,3,2,1,0:T(8,128)(2,1)S(1)}, bf16[6,4,8,64,128]{4,3,2,1,0:T(8,128)(2,1)}, u32[]{:S(2)}) copy-start(bf16[6,4,8,64,128]{4,3,2,1,0:T(8,128)(2,1)} %param.8) | copy-start | bytes 9437188
  157.7 24.2 %all-to-all-start.1 = ((f32[256,1,384]{2,1,0:T(1,128)}), f32[256,1,384]{2,1,0:T(1,128)S(1)}, u32[]{:S(2)}, u32[]{:S(2)}) async-start(f32[256,1,384]{2,1,0:T(1,128)} %broadcast_in_dim.27), calls=%async_computation.1 | async-start | bytes 786432 | tf_op jit(solution)/shard_map/all_to_all | solution.py:194

commit v2 on v1

--- a/solution.py
+++ b/solution.py
@@ -153,6 +153,13 @@
 
 def local_adjoint(grad_normal, normal, totals, hidden_b, weights_b):
     labels = normal.shape[-1]
+    outgoing = jnp.einsum(
+        "dxyzk,dkl->dxyzl",
+        lax.optimization_barrier(hidden_b),
+        weights_b,
+        preferred_element_type=jnp.float32,
+    )
+    normal = outgoing * (labels / totals)
     inner = jnp.sum(grad_normal * normal, axis=-1, keepdims=True)
     grad_out = (labels / totals * (grad_normal - inner / labels)).astype(jnp.bfloat16)
     grad_weights = jnp.einsum(

time: 184 us -> 186 us (1.011)
  other arithmetic: 53.9 us -> 48.2 us
  matrix products: 32.9 us -> 37.7 us
  local copies, waits for them, and re-layouts: 13.4 us -> 17.4 us
    reduce_sum x2 -> x0, other arithmetic: 7.6 us -> none  [local_adjoint(): inner = jnp.sum(grad_normal * normal, axis=-1, keepdims=True)]
    dot_general x0 -> x2, matrix products: none -> 7.52 us  [local_adjoint(): jnp.einsum('dxyzk,dkl->dxyzl', lax.optimization_barrier(hidden_b), weight...]
    all_to_all x1, starting transfers between devices: 21.8 us -> 25.3 us  [all_sum(): lax.all_to_all(rows, axes, 0, 0, tiled=True)]
    dot_general x2, matrix products: 8.14 us -> 5.68 us  [send_terms(): jnp.einsum('dxyzk,dkl->dxyzl', hidden_b, weights_b, preferred_element_typ...]
    ppermute x6, starting transfers between devices: 15 us -> 12.7 us  [trade(): lax.ppermute(jnp.where(odd, high_face, low_face), axis, [(i, i + 1 if i %...]
    unnamed x65 -> x55, local copies, waits for them, and re-layouts: 5.58 us -> 7.91 us
    unnamed x21 -> x19, other arithmetic: 7.16 us -> 7.4 us
where the time goes in v2:
time: 186 us; the launch traced here: 185 us
  starting transfers between devices  55.6 us (30%)
  other arithmetic  48.2 us (26%)
  matrix products  37.7 us (20%)
  waiting for transfers between devices  25 us (13%)
  local copies, waits for them, and re-layouts  17.4 us (9%)
    all_to_all x1, starting transfers between devices, all_sum(): lax.all_to_all(rows, axes, 0, 0, tiled=True)  25.3 us
    dot_general x2, matrix products, local_adjoint(): jnp.einsum('dxyzl,dkl->dxyzk', grad_out, weights_b, preferred_element_typ...  12.8 us
    ppermute x6, starting transfers between devices, trade(): lax.ppermute(jnp.where(odd, high_face, low_face), axis, [(i, i + 1 if i %...  12.7 us
    ppermute x9, starting transfers between devices, trade(): lax.ppermute(jnp.where(odd, low_face, high_face), axis, [(i, i ^ 1) for i...  11.9 us
    dot_general x2, matrix products, local_adjoint(): jnp.einsum('dxyzk,dxyzl->dkl', hidden_b, grad_out, preferred_element_type...  11.6 us
    sub x1, other arithmetic, belief_adjoint(): cotangent - jnp.sum(cotangent * belief, axis=-1, keepdims=True)  11.2 us
    all_to_all x1, waiting for transfers between devices, all_sum(): lax.all_to_all(spread_out, axes, 0, 0, tiled=True).reshape(value.shape)  10.9 us
    all_to_all x1, waiting for transfers between devices, all_sum(): lax.all_to_all(rows, axes, 0, 0, tiled=True)  9.24 us
  transfers between devices with their start and end apart: 17, of which 4 were waited for; matrix products, arithmetic and copies ran while one was open for 19% of the time, Pallas kernels for 0%

profile of v2, /device:TPU:1, one launch (start us, length us, event | category | flops | bytes accessed | tf_op | source)
XLA Modules:
  0.0 185.5 jit_solution(9252688818921281394)
XLA Ops:
  0.6 1.8 fusion.98
  2.5 4.7 %bitcast_dynamic-update-slice_fusion.5 = (bf16[6,4,8,64,128]{4,3,2,1,0:T(8,128)(2,1)S(1)}, f32[4,8,64,128]{3,2,1,0:T(8,128)S(1)}, bf16[6,4,8,64,128]{4,3,2,1,0:T(8,128)(2,1)S(1)}, f32[4,8,64,128]{3,2,1,0:T(8,128)S(1)}) fusion(bf16[6,4,8,64,128]{4,3,2,1,0:T(8,128)(2,1)} %param.7, bf16[4,8,64,128]{3,2,1,0:T(8,128)(2,1)} %param.5, ...), kind=kLoop, calls=%fused_computation.168 | loop fusion | flops 7602174 | bytes 9961472
  7.9 1.2 copy-done
  10.0 0.5 bitcast_dynamic-update-slice_fusion.1
  10.4 1.6 copy-done.25
  12.1 1.9 %fusion.99 = (f32[6,4,8,64]{3,2,1,0:T(8,128)S(1)}, f32[6,4,8,64,128]{4,3,2,1,0:T(8,128)S(1)}) fusion(bf16[6,4,8,64,128]{4,3,2,1,0:T(8,128)(2,1)S(1)} %get-tuple-element.67, bf16[6,128,128]{2,1,0:T(8,128)(2,1)S(1)} %get-tuple-element.42), kind=kOutput, calls=%fused_computation.234 | convolution fusion | flops 404213760 | bytes 9682944 | tf_op jit(solution)/shard_map/dxyzk,dkl->dxyzl/dot_general | solution.py:60
  14.0 2.0 %multiply_convert_fusion = bf16[6,4,8,64,128]{4,3,2,1,0:T(8,128)(2,1)S(1)} fusion(f32[6,4,8,64,128]{4,3,2,1,0:T(8,128)S(1)} %get-tuple-element.64, f32[6,4,8,64]{3,2,1,0:T(8,128)S(1)} %broadcast_divide_fusion.1), kind=kLoop, calls=%fused_computation.11 | loop fusion | flops 3145728 | bytes 9486336 | tf_op jit(solution)/shard_map/convert.29
  16.0 1.7 copy-done.9
  17.7 0.7 select_bitcast_fusion.1
  18.5 3.2 %collective-permute-start = (bf16[1,8,64,128]{3,2,1,0:T(8,128)(2,1)}, bf16[1,8,64,128]{3,2,1,0:T(8,128)(2,1)}, u32[]{:S(2)}, u32[]{:S(2)}) collective-permute-start(bf16[1,8,64,128]{3,2,1,0:T(8,128)(2,1)} %get-tuple-element.25), channel_id=1, source_target_pairs={{0,8},{8,0},{16,24},{24,16},{32,40},{40,32},{48,56},{56,48},{64,72... | collective-permute-start | bytes 393224 | tf_op jit(solution)/shard_map/ppermute | solution.py:72
  21.7 1.9 %collective-permute-start.1 = (bf16[1,8,64,128]{3,2,1,0:T(8,128)(2,1)}, bf16[1,8,64,128]{3,2,1,0:T(8,128)(2,1)}, u32[]{:S(2)}, u32[]{:S(2)}) collective-permute-start(bf16[1,8,64,128]{3,2,1,0:T(8,128)(2,1)} %get-tuple-element.26), channel_id=1, source_target_pairs={{8,16},{16,8},{24,32},{32,24},{40,48},{48,40},{56,64},{64,56},{72,... | collective-permute-start | bytes 393224 | tf_op jit(solution)/shard_map/ppermute | solution.py:76
  23.6 2.8 %slice_bitcast_fusion.13 = (bf16[4,8,64,128]{3,2,1,0:T(8,128)(2,1)S(1)}, bf16[4,8,64,128]{3,2,1,0:T(8,128)(2,1)S(1)}, bf16[4,8,64,128]{3,2,1,0:T(8,128)(2,1)}, bf16[4,8,64,128]{3,2,1,0:T(8,128)(2,1)}) fusion(bf16[6,4,8,64,128]{4,3,2,1,0:T(8,128)(2,1)} %copy-done.9), kind=kLoop, calls=%fused_computation.130 | loop fusion | bytes 4194304 | tf_op jit(solution)/shard_map/convert_element_type | solution.py:219
  26.4 1.1 collective-permute-start.4
  27.5 1.5 broadcast_select_fusion.17
  29.0 1.3 collective-permute-start.2
  30.3 1.3 collective-permute-start.3
  31.6 1.9 %slice_bitcast_fusion.17 = (bf16[3,8,64,128]{3,2,1,0:T(8,128)(2,1)S(1)}, bf16[3,8,64,128]{3,2,1,0:T(8,128)(2,1)}) fusion(bf16[6,4,8,64,128]{4,3,2,1,0:T(8,128)(2,1)} %copy-done.9), kind=kLoop, calls=%fused_computation.178 | loop fusion | bytes 1572864 | tf_op jit(solution)/shard_map/slice | solution.py:104
  33.6 2.0 %bitcast_dynamic-update-slice_fusion = bf16[6,4,8,64,128]{4,3,2,1,0:T(8,128)(2,1)} fusion(bf16[6,4,8,64,128]{4,3,2,1,0:T(8,128)(2,1)} %copy-done.25, f32[4,8,64,128]{3,2,1,0:T(8,128)S(1)} %get-tuple-element.3, bf16[6,4,8,64,128]{4,3,2,1,0:T(8,128)(2,1)} %param.7), kind=kLoop, calls=%fused_computation.163 | loop fusion | flops 786432 | bytes 2097152 | tf_op jit(solution)/shard_map/stack | solution.py:59
  35.6 3.8 %convolution_reduce_fusion = f32[6,4,8,64]{3,2,1,0:T(8,128)S(1)} fusion(bf16[6,4,8,64,128]{4,3,2,1,0:T(8,128)(2,1)} %bitcast_dynamic-update-slice_fusion, bf16[6,128,128]{2,1,0:T(8,128)(2,1)S(1)} %get-tuple-element.42), kind=kOutput, calls=%fused_computation.18 | convolution fusion | flops 404213760 | bytes 3391488 | tf_op jit(solution)/shard_map/dxyzk,dkl->dxyzl/dot_general | solution.py:60
  39.4 0.7 broadcast_divide_fusion
  40.2 1.2 slice.287
  41.5 1.1 slice.286
  42.7 1.0 select_select_fusion.3
  43.7 1.0 select_select_fusion.1
  44.7 1.9 %fusion.91 = (f32[4,8,64]{2,1,0:T(8,128)S(1)}, f32[4,8,64,128]{3,2,1,0:T(8,128)S(1)}) fusion(bf16[4,8,64,128]{3,2,1,0:T(8,128)(2,1)} %param.5, bf16[4,8,1,128]{3,2,1,0:T(2,128)(2,1)S(1)} %get-tuple-element.62, bf16[4,8,63,128]{3,2,1,0:T(8,128)(2,1)S(1)} %slice.293, bf16[4,8,63,128]{3,2,1,0:T(8,128)(2,1)S(1)} %bitcast.360, ...), kind=kLoop, calls=%fused_computation.232 | loop fusion | flops 8386560 | bytes 4726784 | tf_op jit(solution)/shard_map/reduce_sum | solution.py:143
  46.6 11.2 %fusion.35 = (bf16[4,8,64,128]{3,2,1,0:T(8,128)(2,1)S(1)}, f32[4,8,64,128]{3,2,1,0:T(8,128)S(1)}, f32[4,8,64,128]{3,2,1,0:T(8,128)}) fusion(bf16[4,1,64,128]{3,2,1,0:T(8,128)(2,1)S(1)} %get-tuple-element.54, bf16[4,7,64,128]{3,2,1,0:T(8,128)(2,1)S(1)} %slice.287, bf16[4,7,64,128]{3,2,1,0:T(8,128)(2,1)S(1)} %slice.286, ...), kind=kOutput, calls=%fused_computation.74 | output fusion | flops 10225791 | bytes 7880704 | tf_op jit(solution)/shard_map/sub | solution.py:146
  57.8 0.6 multiply_convert_fusion.9
  58.5 0.7 fusion.31
  59.2 0.7 fusion.33
  59.8 0.8 multiply_convert_fusion.7
  61.1 3.2 %collective-permute-start.8 = (bf16[4,1,64,128]{3,2,1,0:T(8,128)(2,1)S(1)}, bf16[4,1,64,128]{3,2,1,0:T(8,128)(2,1)S(1)}, u32[]{:S(2)}, u32[]{:S(2)}) collective-permute-start(bf16[4,1,64,128]{3,2,1,0:T(8,128)(2,1)S(1)} %get-tuple-element.33), channel_id=1, source_target_pairs={{0,2},{2,0},{4,6},{6,4},{1,3},{3,1},{5,7},{7,5},{8,10},{10,8},{12,... | collective-permute-start | bytes 196616 | tf_op jit(solution)/shard_map/ppermute | solution.py:72
  64.3 0.7 collective-permute-start.7
  65.1 3.9 %collective-permute-start.5 = (bf16[1,8,64,128]{3,2,1,0:T(8,128)(2,1)S(1)}, bf16[1,8,64,128]{3,2,1,0:T(8,128)(2,1)S(1)}, u32[]{:S(2)}, u32[]{:S(2)}) collective-permute-start(bf16[1,8,64,128]{3,2,1,0:T(8,128)(2,1)S(1)} %get-tuple-element.36), channel_id=1, source_target_pairs={{8,16},{16,8},{24,32},{32,24},{40,48},{48,40},{56,64},{64,56},{72,... | collective-permute-start | bytes 393224 | tf_op jit(solution)/shard_map/ppermute | solution.py:76
  69.1 2.3 %collective-permute-done.5 = bf16[1,8,64,128]{3,2,1,0:T(8,128)(2,1)S(1)} collective-permute-done((bf16[1,8,64,128]{3,2,1,0:T(8,128)(2,1)S(1)}, bf16[1,8,64,128]{3,2,1,0:T(8,128)(2,1)S(1)}, u32[]{:S(2)}, u32[]{:S(2)}) %collective-permute-start.5) | collective-permute-done | bytes 131104 | tf_op jit(solution)/shard_map/ppermute | solution.py:76
  71.9 0.2 fusion.72
  72.1 1.2 copy-done.13
  73.4 3.8 %fusion.1 = f32[6,4,8,64]{3,2,1,0:T(8,128)S(1)} fusion(bf16[6,4,8,64,128]{4,3,2,1,0:T(8,128)(2,1)S(1)} %fusion.72, f32[6,4,8,64]{3,2,1,0:T(8,128)S(1)} %broadcast_divide_fusion.1, bf16[6,4,8,64,128]{4,3,2,1,0:T(8,128)(2,1)S(1)} %copy-done.13, bf16[6,128,128]{2,1,0:T(8,128)(2,1)S(1)} %copy-done.16), kind=kOutput, calls=%fused_computation.5 | convolution fusion | flops 408932352 | bytes 6586368 | tf_op jit(solution)/shard_map/dxyzk,dkl->dxyzl/dot_general | solution.py:156
  77.1 5.5 %fusion.15 = f32[6,128,128]{2,1,0:T(8,128)S(1)} fusion(bf16[6,4,8,64,128]{4,3,2,1,0:T(8,128)(2,1)S(1)} %copy-done.13, bf16[6,4,8,64,128]{4,3,2,1,0:T(8,128)(2,1)S(1)} %fusion.72, f32[6,4,8,64]{3,2,1,0:T(8,128)S(1)} %broadcast_multiply_fusion.1, f32[6,4,8,64]{3,2,1,0:T(8,128)S(1)} %broadcast_divide_fusion.1), kind=kOutput, calls=%fused_computation.66 | convolution fusion | flops 408944640 | bytes 6782976 | tf_op jit(solution)/shard_map/dxyzk,dxyzl->dkl/dot_general | solution.py:165
  82.7 5.5 %fusion.84 = f32[6,4,8,64,128]{4,3,2,1,0:T(8,128)S(1)} fusion(bf16[6,128,128]{2,1,0:T(8,128)(2,1)S(1)} %copy-done.16, bf16[6,4,8,64,128]{4,3,2,1,0:T(8,128)(2,1)S(1)} %fusion.72, f32[6,4,8,64]{3,2,1,0:T(8,128)S(1)} %broadcast_multiply_fusion.1, f32[6,4,8,64]{3,2,1,0:T(8,128)S(1)} %broadcast_divide_fusion.1), kind=kOutput, calls=%fused_computation.183 | convolution fusion | flops 408944640 | bytes 9732096 | tf_op jit(solution)/shard_map/dxyzl,dkl->dxyzk/dot_general | solution.py:168
  88.2 1.2 multiply_convert_fusion.2
  89.4 0.5 multiply_convert_fusion.1
  89.9 1.7 collective-permute-start.14
  91.7 1.0 multiply_convert_fusion.6
  92.6 1.2 multiply_convert_fusion.3
  94.2 1.1 collective-permute-start.13
  95.3 0.7 collective-permute-start.12
  96.1 4.2 %collective-permute-start.10 = (bf16[1,8,64,128]{3,2,1,0:T(8,128)(2,1)S(1)}, bf16[1,8,64,128]{3,2,1,0:T(8,128)(2,1)S(1)}, u32[]{:S(2)}, u32[]{:S(2)}) collective-permute-start(bf16[1,8,64,128]{3,2,1,0:T(8,128)(2,1)S(1)} %get-tuple-element.30), channel_id=1, source_target_pairs={{8,16},{16,8},{24,32},{32,24},{40,48},{48,40},{56,64},{64,56},{72,... | collective-permute-start | bytes 393224 | tf_op jit(solution)/shard_map/ppermute | solution.py:76
  100.4 2.5 %collective-permute-done.10 = bf16[1,8,64,128]{3,2,1,0:T(8,128)(2,1)S(1)} collective-permute-done((bf16[1,8,64,128]{3,2,1,0:T(8,128)(2,1)S(1)}, bf16[1,8,64,128]{3,2,1,0:T(8,128)(2,1)S(1)}, u32[]{:S(2)}, u32[]{:S(2)}) %collective-permute-start.10) | collective-permute-done | bytes 131104 | tf_op jit(solution)/shard_map/ppermute | solution.py:76
  103.4 0.2 fusion.78
  103.6 0.2 copy-done.23
  103.8 1.1 copy-done.26
  104.9 3.8 %fusion.4 = f32[6,4,8,64]{3,2,1,0:T(8,128)S(1)} fusion(bf16[6,4,8,64,128]{4,3,2,1,0:T(8,128)(2,1)S(1)} %fusion.78, f32[6,4,8,64]{3,2,1,0:T(8,128)S(1)} %copy-done.23, bf16[6,4,8,64,128]{4,3,2,1,0:T(8,128)(2,1)S(1)} %copy-done.26, bf16[6,128,128]{2,1,0:T(8,128)(2,1)S(1)} %copy-done.16), kind=kOutput, calls=%fused_computation.8 | convolution fusion | flops 408932352 | bytes 6586368 | tf_op jit(solution)/shard_map/dxyzk,dkl->dxyzl/dot_general | solution.py:156
  108.7 6.1 %fusion.25 = f32[6,128,128]{2,1,0:T(8,128)} fusion(f32[6,128,128]{2,1,0:T(8,128)S(1)} %fusion.15, bf16[6,4,8,64,128]{4,3,2,1,0:T(8,128)(2,1)S(1)} %copy-done.26, bf16[6,4,8,64,128]{4,3,2,1,0:T(8,128)(2,1)S(1)} %fusion.78, f32[6,4,8,64]{3,2,1,0:T(8,128)S(1)} %broadcast_multiply_fusion, f32[6,4,8,64]{3,2,1,0:T(8,128)S(1)} %copy-done.23), kind=kOutput, calls=%fused_computation.68 | convolution fusion | flops 409042944 | bytes 7176192 | tf_op jit(solution)/shard_map/dxyzk,dxyzl->dkl/dot_general | solution.py:165
  114.8 25.3 %all-to-all-start = ((f32[256,1,384]{2,1,0:T(1,128)}), f32[256,1,384]{2,1,0:T(1,128)}, u32[]{:S(2)}, u32[]{:S(2)}) async-start(f32[256,1,384]{2,1,0:T(1,128)} %bitcast.75), calls=%async_computation | async-start | bytes 786432 | tf_op jit(solution)/shard_map/all_to_all | solution.py:198
  140.1 0.8 reshape.80
  141.0 7.3 %fusion.80 = f32[6,4,8,64,128]{4,3,2,1,0:T(8,128)} fusion(bf16[6,128,128]{2,1,0:T(8,128)(2,1)S(1)} %copy-done.16, bf16[6,4,8,64,128]{4,3,2,1,0:T(8,128)(2,1)} %copy-done.14, f32[6,4,8,64]{3,2,1,0:T(8,128)S(1)} %broadcast_multiply_fusion, f32[6,4,8,64]{3,2,1,0:T(8,128)S(1)} %copy-done.24), kind=kOutput, calls=%fused_computation.179 | convolution fusion | flops 408944640 | bytes 9732096 | tf_op jit(solution)/shard_map/dxyzl,dkl->dxyzk/dot_general | solution.py:168
  148.3 9.2 %all-to-all-done = f32[256,1,384]{2,1,0:T(1,128)} async-done(((f32[256,1,384]{2,1,0:T(1,128)}), f32[256,1,384]{2,1,0:T(1,128)}, u32[]{:S(2)}, u32[]{:S(2)}) %all-to-all-start) | async-done | bytes 393248 | tf_op jit(solution)/shard_map/all_to_all | solution.py:198
  157.5 1.3 reduce_sum.69
  158.8 0.7 multiply_reduce_fusion
  159.6 1.0 broadcast_in_dim.27
  160.5 5.7 %all-to-all-start.1 = ((f32[256,1,384]{2,1,0:T(1,128)}), f32[256,1,384]{2,1,0:T(1,128)S(1)}, u32[]{:S(2)}, u32[]{:S(2)}) async-start(f32[256,1,384]{2,1,0:T(1,128)} %broadcast_in_dim.27), calls=%async_computation.1 | async-start | bytes 786432 | tf_op jit(solution)/shard_map/all_to_all | solution.py:201
  166.2 7.6 %fusion.50 = f32[4,8,64,128]{3,2,1,0:T(8,128)} fusion(f32[6,4,8,64,128]{4,3,2,1,0:T(8,128)} %fusion.80, f32[4,8,64,128]{3,2,1,0:T(8,128)} %copy-done.5, f32[4,8,64,128]{3,2,1,0:T(8,128)} %get-tuple-element.65, bf16[4,8,64,128]{3,2,1,0:T(8,128)(2,1)} %param.5, f32[4,8,64,128]{3,2,1,0:T(8,128)} %copy-done.7, f32[4,8,64,128]{3,2,1,0:T(8,128)} %copy-done.10, ...), kind=kLoop, calls=%fused_computation.89 | loop fusion | flops 12320768 | bytes 19922944 | tf_op jit(solution)/shard_map/mul | solution.py:240
  173.8 10.9 %all-to-all-done.1 = f32[256,1,384]{2,1,0:T(1,128)S(1)} async-done(((f32[256,1,384]{2,1,0:T(1,128)}), f32[256,1,384]{2,1,0:T(1,128)S(1)}, u32[]{:S(2)}, u32[]{:S(2)}) %all-to-all-start.1) | async-done | bytes 393248 | tf_op jit(solution)/shard_map/all_to_all | solution.py:201
  184.7 0.7 copy.56
  (112 shorter events, 3.8 us)
Async XLA Ops:
  2.5 33.1 %copy-start.15 = (bf16[6,128,128]{2,1,0:T(8,128)(2,1)}, bf16[6,128,128]{2,1,0:T(8,128)(2,1)S(1)}, u32[]{:S(2)}) copy-start(bf16[6,128,128]{2,1,0:T(8,128)(2,1)S(1)} %get-tuple-element.42) | copy-start | bytes 589828
  2.5 4.7 %copy-start.4 = (bf16[6,4,8,64,128]{4,3,2,1,0:T(8,128)(2,1)S(1)}, bf16[6,4,8,64,128]{4,3,2,1,0:T(8,128)(2,1)}, u32[]{:S(2)}) copy-start(bf16[6,4,8,64,128]{4,3,2,1,0:T(8,128)(2,1)} %param.7) | copy-start | bytes 9437188
  7.2 1.9 %copy-start = (bf16[6,4,8,64,128]{4,3,2,1,0:T(8,128)(2,1)S(1)}, bf16[6,4,8,64,128]{4,3,2,1,0:T(8,128)(2,1)}, u32[]{:S(2)}) copy-start(bf16[6,4,8,64,128]{4,3,2,1,0:T(8,128)(2,1)} %param.8) | copy-start | bytes 9437188
  10.4 1.7 copy-start.25
  10.4 3.5 %copy-start.12 = (bf16[6,4,8,64,128]{4,3,2,1,0:T(8,128)(2,1)}, bf16[6,4,8,64,128]{4,3,2,1,0:T(8,128)(2,1)S(1)}, u32[]{:S(2)}) copy-start(bf16[6,4,8,64,128]{4,3,2,1,0:T(8,128)(2,1)S(1)} %get-tuple-element.67) | copy-start | bytes 9437188
  16.0 1.7 copy-start.9
  18.5 25.2 %collective-permute-start = (bf16[1,8,64,128]{3,2,1,0:T(8,128)(2,1)}, bf16[1,8,64,128]{3,2,1,0:T(8,128)(2,1)}, u32[]{:S(2)}, u32[]{:S(2)}) collective-permute-start(bf16[1,8,64,128]{3,2,1,0:T(8,128)(2,1)} %get-tuple-element.25), channel_id=1, source_target_pairs={{0,8},{8,0},{16,24},{24,16},{32,40},{40,32},{48,56},{56,48},{64,72... | collective-permute-start | bytes 393224 | tf_op jit(solution)/shard_map/ppermute | solution.py:72
  21.7 22.0 %collective-permute-start.1 = (bf16[1,8,64,128]{3,2,1,0:T(8,128)(2,1)}, bf16[1,8,64,128]{3,2,1,0:T(8,128)(2,1)}, u32[]{:S(2)}, u32[]{:S(2)}) collective-permute-start(bf16[1,8,64,128]{3,2,1,0:T(8,128)(2,1)} %get-tuple-element.26), channel_id=1, source_target_pairs={{8,16},{16,8},{24,32},{32,24},{40,48},{48,40},{56,64},{64,56},{72,... | collective-permute-start | bytes 393224 | tf_op jit(solution)/shard_map/ppermute | solution.py:76
  26.3 4.0 %copy-start.17 = (bf16[4,8,64,128]{3,2,1,0:T(8,128)(2,1)}, bf16[4,8,64,128]{3,2,1,0:T(8,128)(2,1)S(1)}, u32[]{:S(2)}) copy-start(bf16[4,8,64,128]{3,2,1,0:T(8,128)(2,1)S(1)} %get-tuple-element.19) | copy-start | bytes 1572868
  26.4 16.2 %collective-permute-start.4 = (bf16[4,8,1,128]{3,2,1,0:T(2,128)(2,1)S(1)}, bf16[4,8,1,128]{3,2,1,0:T(2,128)(2,1)S(1)}, u32[]{:S(2)}, u32[]{:S(2)}) collective-permute-start(bf16[4,8,1,128]{3,2,1,0:T(2,128)(2,1)S(1)} %broadcast_select_fusion.27), channel_id=1, source_target_pairs={{0,1},{1,0},{2,3},{3,2},{4,5},{5,4},{6,7},{7,6},{8,9},{9,8},{10,11... | collective-permute-start | bytes 24584 | tf_op jit(solution)/shard_map/ppermute | solution.py:72
  29.0 13.6 %collective-permute-start.2 = (bf16[4,1,64,128]{3,2,1,0:T(8,128)(2,1)}, bf16[4,1,64,128]{3,2,1,0:T(8,128)(2,1)}, u32[]{:S(2)}, u32[]{:S(2)}) collective-permute-start(bf16[4,1,64,128]{3,2,1,0:T(8,128)(2,1)} %get-tuple-element.37), channel_id=1, source_target_pairs={{0,2},{2,0},{4,6},{6,4},{1,3},{3,1},{5,7},{7,5},{8,10},{10,8},{12,... | collective-permute-start | bytes 196616 | tf_op jit(solution)/shard_map/ppermute | solution.py:72
  30.3 12.3 %collective-permute-start.3 = (bf16[4,1,64,128]{3,2,1,0:T(8,128)(2,1)}, bf16[4,1,64,128]{3,2,1,0:T(8,128)(2,1)}, u32[]{:S(2)}, u32[]{:S(2)}) collective-permute-start(bf16[4,1,64,128]{3,2,1,0:T(8,128)(2,1)} %get-tuple-element.38), channel_id=1, source_target_pairs={{2,4},{4,2},{3,5},{5,3},{10,12},{12,10},{11,13},{13,11},{18,20},{2... | collective-permute-start | bytes 196616 | tf_op jit(solution)/shard_map/ppermute | solution.py:76
  35.6 4.5 %copy-start.18 = (bf16[4,8,64,128]{3,2,1,0:T(8,128)(2,1)S(1)}, bf16[4,8,64,128]{3,2,1,0:T(8,128)(2,1)}, u32[]{:S(2)}) copy-start(bf16[4,8,64,128]{3,2,1,0:T(8,128)(2,1)} %copy-done.17) | copy-start | bytes 1572868
  40.2 19.6 %copy-start.3 = (bf16[4,8,63,128]{3,2,1,0:T(8,128)(2,1)}, bf16[4,8,63,128]{3,2,1,0:T(8,128)(2,1)S(1)}, u32[]{:S(2)}) copy-start(bf16[4,8,63,128]{3,2,1,0:T(8,128)(2,1)S(1)} %slice.293) | copy-start | bytes 1548292
  42.5 4.1 %copy-start.8 = (bf16[3,8,64,128]{3,2,1,0:T(8,128)(2,1)S(1)}, bf16[3,8,64,128]{3,2,1,0:T(8,128)(2,1)}, u32[]{:S(2)}) copy-start(bf16[3,8,64,128]{3,2,1,0:T(8,128)(2,1)} %get-tuple-element.24) | copy-start | bytes 1179652
  42.6 4.1 %copy-start.11 = (bf16[4,8,64,128]{3,2,1,0:T(8,128)(2,1)S(1)}, bf16[4,8,64,128]{3,2,1,0:T(8,128)(2,1)}, u32[]{:S(2)}) copy-start(bf16[4,8,64,128]{3,2,1,0:T(8,128)(2,1)} %param.5) | copy-start | bytes 1572868
  42.6 4.1 %copy-start.22 = (f32[4,8,64,128]{3,2,1,0:T(8,128)S(1)}, f32[4,8,64,128]{3,2,1,0:T(8,128)}, u32[]{:S(2)}) copy-start(f32[4,8,64,128]{3,2,1,0:T(8,128)} %param.9) | copy-start | bytes 3145732
  46.6 13.2 %copy-start.7 = (f32[4,8,64,128]{3,2,1,0:T(8,128)}, f32[4,8,64,128]{3,2,1,0:T(8,128)S(1)}, u32[]{:S(2)}) copy-start(f32[4,8,64,128]{3,2,1,0:T(8,128)S(1)} %get-tuple-element.13) | copy-start | bytes 3145732
  58.5 2.4 %copy-start.20 = (bf16[4,8,64,128]{3,2,1,0:T(8,128)(2,1)}, bf16[4,8,64,128]{3,2,1,0:T(8,128)(2,1)S(1)}, u32[]{:S(2)}) copy-start(bf16[4,8,64,128]{3,2,1,0:T(8,128)(2,1)S(1)} %multiply_convert_fusion.9) | copy-start | bytes 1572868
  59.1 1.9 %copy-start.19 = (bf16[4,8,64,128]{3,2,1,0:T(8,128)(2,1)}, bf16[4,8,64,128]{3,2,1,0:T(8,128)(2,1)S(1)}, u32[]{:S(2)}) copy-start(bf16[4,8,64,128]{3,2,1,0:T(8,128)(2,1)S(1)} %fusion.31) | copy-start | bytes 1572868
  60.6 8.4 %collective-permute-start.9 = (bf16[4,8,1,128]{3,2,1,0:T(2,128)(2,1)S(1)}, bf16[4,8,1,128]{3,2,1,0:T(2,128)(2,1)S(1)}, u32[]{:S(2)}, u32[]{:S(2)}) collective-permute-start(bf16[4,8,1,128]{3,2,1,0:T(2,128)(2,1)S(1)} %broadcast_select_fusion.24), channel_id=1, source_target_pairs={{0,1},{1,0},{2,3},{3,2},{4,5},{5,4},{6,7},{7,6},{8,9},{9,8},{10,11... | collective-permute-start | bytes 24584 | tf_op jit(solution)/shard_map/ppermute | solution.py:72
  60.9 10.8 %slice-start.1 = ((bf16[4,8,64,128]{3,2,1,0:T(8,128)(2,1)}), bf16[4,7,64,128]{3,2,1,0:T(8,128)(2,1)S(1)}, s32[]{:S(2)}) async-start(bf16[4,8,64,128]{3,2,1,0:T(8,128)(2,1)} %copy-done.20), calls=%async_computation.3 | async-start | bytes 917504 | tf_op jit(solution)/shard_map/slice | solution.py:128
  61.1 10.5 %slice-start = ((bf16[4,8,64,128]{3,2,1,0:T(8,128)(2,1)}), bf16[3,8,64,128]{3,2,1,0:T(8,128)(2,1)S(1)}, s32[]{:S(2)}) async-start(bf16[4,8,64,128]{3,2,1,0:T(8,128)(2,1)} %copy-done.19), calls=%async_computation.2 | async-start | bytes 786432 | tf_op jit(solution)/shard_map/slice | solution.py:133
  61.1 7.9 %collective-permute-start.8 = (bf16[4,1,64,128]{3,2,1,0:T(8,128)(2,1)S(1)}, bf16[4,1,64,128]{3,2,1,0:T(8,128)(2,1)S(1)}, u32[]{:S(2)}, u32[]{:S(2)}) collective-permute-start(bf16[4,1,64,128]{3,2,1,0:T(8,128)(2,1)S(1)} %get-tuple-element.33), channel_id=1, source_target_pairs={{0,2},{2,0},{4,6},{6,4},{1,3},{3,1},{5,7},{7,5},{8,10},{10,8},{12,... | collective-permute-start | bytes 196616 | tf_op jit(solution)/shard_map/ppermute | solution.py:72
  64.3 4.8 %collective-permute-start.7 = (bf16[4,1,64,128]{3,2,1,0:T(8,128)(2,1)S(1)}, bf16[4,1,64,128]{3,2,1,0:T(8,128)(2,1)S(1)}, u32[]{:S(2)}, u32[]{:S(2)}) collective-permute-start(bf16[4,1,64,128]{3,2,1,0:T(8,128)(2,1)S(1)} %get-tuple-element.34), channel_id=1, source_target_pairs={{2,4},{4,2},{3,5},{5,3},{10,12},{12,10},{11,13},{13,11},{18,20},{2... | collective-permute-start | bytes 196616 | tf_op jit(solution)/shard_map/ppermute | solution.py:76
  65.0 4.2 %collective-permute-start.6 = (bf16[1,8,64,128]{3,2,1,0:T(8,128)(2,1)S(1)}, bf16[1,8,64,128]{3,2,1,0:T(8,128)(2,1)S(1)}, u32[]{:S(2)}, u32[]{:S(2)}) collective-permute-start(bf16[1,8,64,128]{3,2,1,0:T(8,128)(2,1)S(1)} %get-tuple-element.35), channel_id=1, source_target_pairs={{0,8},{8,0},{16,24},{24,16},{32,40},{40,32},{48,56},{56,48},{64,72... | collective-permute-start | bytes 393224 | tf_op jit(solution)/shard_map/ppermute | solution.py:72
  65.1 6.4 %collective-permute-start.5 = (bf16[1,8,64,128]{3,2,1,0:T(8,128)(2,1)S(1)}, bf16[1,8,64,128]{3,2,1,0:T(8,128)(2,1)S(1)}, u32[]{:S(2)}, u32[]{:S(2)}) collective-permute-start(bf16[1,8,64,128]{3,2,1,0:T(8,128)(2,1)S(1)} %get-tuple-element.36), channel_id=1, source_target_pairs={{8,16},{16,8},{24,32},{32,24},{40,48},{48,40},{56,64},{64,56},{72,... | collective-permute-start | bytes 393224 | tf_op jit(solution)/shard_map/ppermute | solution.py:76
  71.5 1.9 %copy-start.13 = (bf16[6,4,8,64,128]{4,3,2,1,0:T(8,128)(2,1)S(1)}, bf16[6,4,8,64,128]{4,3,2,1,0:T(8,128)(2,1)}, u32[]{:S(2)}) copy-start(bf16[6,4,8,64,128]{4,3,2,1,0:T(8,128)(2,1)} %copy-done.12) | copy-start | bytes 9437188
  71.5 1.9 %copy-start.16 = (bf16[6,128,128]{2,1,0:T(8,128)(2,1)S(1)}, bf16[6,128,128]{2,1,0:T(8,128)(2,1)}, u32[]{:S(2)}) copy-start(bf16[6,128,128]{2,1,0:T(8,128)(2,1)} %copy-done.15) | copy-start | bytes 589828
  82.7 5.5 %copy-start.1 = (bf16[6,4,8,64,128]{4,3,2,1,0:T(8,128)(2,1)S(1)}, bf16[6,4,8,64,128]{4,3,2,1,0:T(8,128)(2,1)}, u32[]{:S(2)}) copy-start(bf16[6,4,8,64,128]{4,3,2,1,0:T(8,128)(2,1)} %param.8) | copy-start | bytes 9437188
  89.4 3.2 %copy-start.10 = (f32[4,8,64,128]{3,2,1,0:T(8,128)}, f32[4,8,64,128]{3,2,1,0:T(8,128)S(1)}, u32[]{:S(2)}) copy-start(f32[4,8,64,128]{3,2,1,0:T(8,128)S(1)} %get-tuple-element.5) | copy-start | bytes 3145732
  89.4 3.2 %copy-start.5 = (f32[4,8,64,128]{3,2,1,0:T(8,128)}, f32[4,8,64,128]{3,2,1,0:T(8,128)S(1)}, u32[]{:S(2)}) copy-start(f32[4,8,64,128]{3,2,1,0:T(8,128)S(1)} %get-tuple-element.7) | copy-start | bytes 3145732
  89.9 2.7 %copy-start.6 = (f32[4,8,64,128]{3,2,1,0:T(8,128)}, f32[4,8,64,128]{3,2,1,0:T(8,128)S(1)}, u32[]{:S(2)}) copy-start(f32[4,8,64,128]{3,2,1,0:T(8,128)S(1)} %get-tuple-element.9) | copy-start | bytes 3145732
  89.9 10.3 %collective-permute-start.14 = (bf16[4,8,1,128]{3,2,1,0:T(2,128)(2,1)S(1)}, bf16[4,8,1,128]{3,2,1,0:T(2,128)(2,1)S(1)}, u32[]{:S(2)}, u32[]{:S(2)}) collective-permute-start(bf16[4,8,1,128]{3,2,1,0:T(2,128)(2,1)S(1)} %broadcast_select_fusion.21), channel_id=1, source_target_pairs={{0,1},{1,0},{2,3},{3,2},{4,5},{5,4},{6,7},{7,6},{8,9},{9,8},{10,11... | collective-permute-start | bytes 24584 | tf_op jit(solution)/shard_map/ppermute | solution.py:72
  94.2 6.1 %collective-permute-start.13 = (bf16[4,1,64,128]{3,2,1,0:T(8,128)(2,1)S(1)}, bf16[4,1,64,128]{3,2,1,0:T(8,128)(2,1)S(1)}, u32[]{:S(2)}, u32[]{:S(2)}) collective-permute-start(bf16[4,1,64,128]{3,2,1,0:T(8,128)(2,1)S(1)} %get-tuple-element.27), channel_id=1, source_target_pairs={{0,2},{2,0},{4,6},{6,4},{1,3},{3,1},{5,7},{7,5},{8,10},{10,8},{12,... | collective-permute-start | bytes 196616 | tf_op jit(solution)/shard_map/ppermute | solution.py:72
  95.3 5.0 %collective-permute-start.12 = (bf16[4,1,64,128]{3,2,1,0:T(8,128)(2,1)S(1)}, bf16[4,1,64,128]{3,2,1,0:T(8,128)(2,1)S(1)}, u32[]{:S(2)}, u32[]{:S(2)}) collective-permute-start(bf16[4,1,64,128]{3,2,1,0:T(8,128)(2,1)S(1)} %get-tuple-element.28), channel_id=1, source_target_pairs={{2,4},{4,2},{3,5},{5,3},{10,12},{12,10},{11,13},{13,11},{18,20},{2... | collective-permute-start | bytes 196616 | tf_op jit(solution)/shard_map/ppermute | solution.py:76
  96.0 4.4 %collective-permute-start.11 = (bf16[1,8,64,128]{3,2,1,0:T(8,128)(2,1)S(1)}, bf16[1,8,64,128]{3,2,1,0:T(8,128)(2,1)S(1)}, u32[]{:S(2)}, u32[]{:S(2)}) collective-permute-start(bf16[1,8,64,128]{3,2,1,0:T(8,128)(2,1)S(1)} %get-tuple-element.29), channel_id=1, source_target_pairs={{0,8},{8,0},{16,24},{24,16},{32,40},{40,32},{48,56},{56,48},{64,72... | collective-permute-start | bytes 393224 | tf_op jit(solution)/shard_map/ppermute | solution.py:72
  96.1 6.8 %collective-permute-start.10 = (bf16[1,8,64,128]{3,2,1,0:T(8,128)(2,1)S(1)}, bf16[1,8,64,128]{3,2,1,0:T(8,128)(2,1)S(1)}, u32[]{:S(2)}, u32[]{:S(2)}) collective-permute-start(bf16[1,8,64,128]{3,2,1,0:T(8,128)(2,1)S(1)} %get-tuple-element.30), channel_id=1, source_target_pairs={{8,16},{16,8},{24,32},{32,24},{40,48},{48,40},{56,64},{64,56},{72,... | collective-permute-start | bytes 393224 | tf_op jit(solution)/shard_map/ppermute | solution.py:76
  102.9 0.9 copy-start.23
  102.9 1.9 %copy-start.26 = (bf16[6,4,8,64,128]{4,3,2,1,0:T(8,128)(2,1)S(1)}, bf16[6,4,8,64,128]{4,3,2,1,0:T(8,128)(2,1)}, u32[]{:S(2)}) copy-start(bf16[6,4,8,64,128]{4,3,2,1,0:T(8,128)(2,1)} %bitcast_dynamic-update-slice_fusion) | copy-start | bytes 9437188
  104.9 3.8 %copy-start.14 = (bf16[6,4,8,64,128]{4,3,2,1,0:T(8,128)(2,1)}, bf16[6,4,8,64,128]{4,3,2,1,0:T(8,128)(2,1)S(1)}, u32[]{:S(2)}) copy-start(bf16[6,4,8,64,128]{4,3,2,1,0:T(8,128)(2,1)S(1)} %fusion.78) | copy-start | bytes 9437188
  108.7 31.4 %copy-start.21 = (f32[6,128,128]{2,1,0:T(8,128)S(1)}, f32[6,128,128]{2,1,0:T(8,128)}, u32[]{:S(2)}) copy-start(f32[6,128,128]{2,1,0:T(8,128)} %get-tuple-element.41) | copy-start | bytes 1179652
  108.7 32.3 %copy-start.24 = (f32[6,4,8,64]{3,2,1,0:T(8,128)S(1)}, f32[6,4,8,64]{3,2,1,0:T(8,128)}, u32[]{:S(2)}) copy-start(f32[6,4,8,64]{3,2,1,0:T(8,128)} %broadcast_divide_fusion) | copy-start | bytes 147460
  114.8 42.7 %all-to-all-start = ((f32[256,1,384]{2,1,0:T(1,128)}), f32[256,1,384]{2,1,0:T(1,128)}, u32[]{:S(2)}, u32[]{:S(2)}) async-start(f32[256,1,384]{2,1,0:T(1,128)} %bitcast.75), calls=%async_computation | async-start | bytes 786432 | tf_op jit(solution)/shard_map/all_to_all | solution.py:198
  141.0 25.3 %copy-start.2 = (bf16[6,4,8,64,128]{4,3,2,1,0:T(8,128)(2,1)S(1)}, bf16[6,4,8,64,128]{4,3,2,1,0:T(8,128)(2,1)}, u32[]{:S(2)}) copy-start(bf16[6,4,8,64,128]{4,3,2,1,0:T(8,128)(2,1)} %param.8) | copy-start | bytes 9437188
  160.5 24.2 %all-to-all-start.1 = ((f32[256,1,384]{2,1,0:T(1,128)}), f32[256,1,384]{2,1,0:T(1,128)S(1)}, u32[]{:S(2)}, u32[]{:S(2)}) async-start(f32[256,1,384]{2,1,0:T(1,128)} %broadcast_in_dim.27), calls=%async_computation.1 | async-start | bytes 786432 | tf_op jit(solution)/shard_map/all_to_all | solution.py:201

commit v3 on v1

--- a/solution.py
+++ b/solution.py
@@ -225,11 +225,11 @@
     weights_one, grad_hidden_one = local_adjoint(
         grad_normal_one, normal_one, totals_one, hidden_one, weights_b
     )
-    ratios_one = [grad_hidden_one[OPPOSE[index]] / first[index] for index in range(6)]
-    total_one = ratios_one[0]
+    others_one = except_products(first)
+    total_one = grad_hidden_one[OPPOSE[0]] * others_one[0]
     for index in range(1, 6):
-        total_one = total_one + ratios_one[index]
-    grad_potential = grad_potential + whole_one * total_one
+        total_one = total_one + grad_hidden_one[OPPOSE[index]] * others_one[index]
+    grad_potential = grad_potential + total_one
     grad_unary = potential * grad_potential
     grad_compat = all_sum(weights_two + weights_one, weights, ("gx", "gy", "gz"))
     return (grad_unary, grad_compat)

time: 184 us -> 182 us (0.989)
  other arithmetic: 53.9 us -> 49.5 us
  waiting for transfers between devices: 25 us -> 28.4 us
    all_to_all x1, waiting for transfers between devices: 9.37 us -> 17.5 us  [all_sum(): lax.all_to_all(rows, axes, 0, 0, tiled=True)]
    all_to_all x1, waiting for transfers between devices: 10.9 us -> 6.21 us  [all_sum(): lax.all_to_all(spread_out, axes, 0, 0, tiled=True).reshape(value.shape)]
    mul x1, other arithmetic: 7.56 us -> 4.14 us  [body(): grad_unary = potential * grad_potential]
    unnamed x65 -> x73, local copies, waits for them, and re-layouts: 5.58 us -> 5.66 us
  transfers between devices with their start and end apart: 17 -> 17, of which waited for: 4 -> 4; matrix products, arithmetic and copies ran while one was open for 19% -> 17% of each run, Pallas kernels for 0% -> 0%
where the time goes in v3:
time: 182 us; the launch traced here: 181 us
  starting transfers between devices  54.8 us (30%)
  other arithmetic  49.5 us (27%)
  matrix products  33.6 us (18%)
  waiting for transfers between devices  28.4 us (16%)
  local copies, waits for them, and re-layouts  13.3 us (7%)
  between operations  1.84 us (1%)
    all_to_all x1, starting transfers between devices, all_sum(): lax.all_to_all(rows, axes, 0, 0, tiled=True)  20.9 us
    all_to_all x1, waiting for transfers between devices, all_sum(): lax.all_to_all(rows, axes, 0, 0, tiled=True)  17.5 us
    ppermute x6, starting transfers between devices, trade(): lax.ppermute(jnp.where(odd, high_face, low_face), axis, [(i, i + 1 if i %...  15 us
    dot_general x2, matrix products, local_adjoint(): jnp.einsum('dxyzl,dkl->dxyzk', grad_out, weights_b, preferred_element_typ...  13.5 us
    ppermute x9, starting transfers between devices, trade(): lax.ppermute(jnp.where(odd, low_face, high_face), axis, [(i, i ^ 1) for i...  13.2 us
    dot_general x2, matrix products, local_adjoint(): jnp.einsum('dxyzk,dxyzl->dkl', hidden_b, grad_out, preferred_element_type...  11.9 us
    sub x1, other arithmetic, belief_adjoint(): cotangent - jnp.sum(cotangent * belief, axis=-1, keepdims=True)  11.2 us
    dot_general x2, matrix products, send_terms(): jnp.einsum('dxyzk,dkl->dxyzl', hidden_b, weights_b, preferred_element_typ...  8.15 us
  transfers between devices with their start and end apart: 17, of which 4 were waited for; matrix products, arithmetic and copies ran while one was open for 17% of the time, Pallas kernels for 0%

profile of v3, /device:TPU:1, one launch (start us, length us, event | category | flops | bytes accessed | tf_op | source)
XLA Modules:
  0.0 181.4 jit_solution(4525822210707255120)
XLA Ops:
  0.7 4.7 %bitcast_dynamic-update-slice_fusion.5 = (bf16[6,4,8,64,128]{4,3,2,1,0:T(8,128)(2,1)S(1)}, f32[4,8,64,128]{3,2,1,0:T(8,128)S(1)}, bf16[6,4,8,64,128]{4,3,2,1,0:T(8,128)(2,1)S(1)}, f32[4,8,64,128]{3,2,1,0:T(8,128)S(1)}) fusion(bf16[6,4,8,64,128]{4,3,2,1,0:T(8,128)(2,1)} %param.7, bf16[4,8,64,128]{3,2,1,0:T(8,128)(2,1)} %param.5, ...), kind=kLoop, calls=%fused_computation.172 | loop fusion | flops 7602174 | bytes 9961472
  6.3 1.2 copy-done.4
  7.7 0.2 bitcast_dynamic-update-slice_fusion.3
  8.4 0.3 copy-done.31
  8.7 0.8 fusion.102
  9.5 0.4 bitcast_dynamic-update-slice_fusion
  10.0 1.6 copy-done.19
  11.6 1.9 %fusion.103 = (f32[6,4,8,64]{3,2,1,0:T(8,128)S(1)}, f32[6,4,8,64,128]{4,3,2,1,0:T(8,128)S(1)}) fusion(bf16[6,4,8,64,128]{4,3,2,1,0:T(8,128)(2,1)S(1)} %get-tuple-element.69, bf16[6,128,128]{2,1,0:T(8,128)(2,1)S(1)} %get-tuple-element.42), kind=kOutput, calls=%fused_computation.237 | convolution fusion | flops 404213760 | bytes 9682944 | tf_op jit(solution)/shard_map/dxyzk,dkl->dxyzl/dot_general | solution.py:60
  13.5 2.0 %multiply_convert_fusion = bf16[6,4,8,64,128]{4,3,2,1,0:T(8,128)(2,1)S(1)} fusion(f32[6,4,8,64,128]{4,3,2,1,0:T(8,128)S(1)} %get-tuple-element.64, f32[6,4,8,64]{3,2,1,0:T(8,128)S(1)} %broadcast_divide_fusion.1), kind=kLoop, calls=%fused_computation.11 | loop fusion | flops 3145728 | bytes 9486336 | tf_op jit(solution)/shard_map/convert.29
  15.6 0.6 copy-done.3
  16.2 1.1 slice_bitcast_fusion.13
  17.3 0.8 copy-done.12
  18.1 0.7 broadcast_select_fusion.27
  18.8 2.5 %collective-permute-start.4 = (bf16[4,8,1,128]{3,2,1,0:T(2,128)(2,1)}, bf16[4,8,1,128]{3,2,1,0:T(2,128)(2,1)S(1)}, u32[]{:S(2)}, u32[]{:S(2)}) collective-permute-start(bf16[4,8,1,128]{3,2,1,0:T(2,128)(2,1)} %broadcast_select_fusion.27), channel_id=1, source_target_pairs={{0,1},{1,0},{2,3},{3,2},{4,5},{5,4},{6,7},{7,6},{8,9},{9,8},{10,11... | collective-permute-start | bytes 24584 | tf_op jit(solution)/shard_map/ppermute | solution.py:72
  21.3 1.7 select_bitcast_fusion.1
  23.0 1.0 collective-permute-start
  23.9 3.0 %collective-permute-start.1 = (bf16[1,8,64,128]{3,2,1,0:T(8,128)(2,1)}, bf16[1,8,64,128]{3,2,1,0:T(8,128)(2,1)}, u32[]{:S(2)}, u32[]{:S(2)}) collective-permute-start(bf16[1,8,64,128]{3,2,1,0:T(8,128)(2,1)} %get-tuple-element.26), channel_id=1, source_target_pairs={{8,16},{16,8},{24,32},{32,24},{40,48},{48,40},{56,64},{64,56},{72,... | collective-permute-start | bytes 393224 | tf_op jit(solution)/shard_map/ppermute | solution.py:76
  26.9 1.5 broadcast_select_fusion.17
  28.5 1.3 collective-permute-start.2
  29.7 1.3 collective-permute-start.3
  31.0 1.9 %slice_bitcast_fusion.17 = (bf16[3,8,64,128]{3,2,1,0:T(8,128)(2,1)}, bf16[3,8,64,128]{3,2,1,0:T(8,128)(2,1)S(1)}) fusion(bf16[6,4,8,64,128]{4,3,2,1,0:T(8,128)(2,1)} %copy-done.12), kind=kLoop, calls=%fused_computation.182 | loop fusion | bytes 1572864 | tf_op jit(solution)/shard_map/slice | solution.py:104
  33.0 6.3 %fusion.104 = (f32[6,4,8,64]{3,2,1,0:T(8,128)S(1)}, f32[6,4,8,64,128]{4,3,2,1,0:T(8,128)}) fusion(bf16[6,4,8,64,128]{4,3,2,1,0:T(8,128)(2,1)} %copy-done.19, bf16[6,128,128]{2,1,0:T(8,128)(2,1)S(1)} %get-tuple-element.42), kind=kOutput, calls=%fused_computation.238 | convolution fusion | flops 404213760 | bytes 9682944 | tf_op jit(solution)/shard_map/dxyzk,dkl->dxyzl/dot_general | solution.py:60
  39.5 1.1 slice.286
  40.5 1.1 slice.287
  41.7 1.0 select_select_fusion.3
  42.7 1.0 select_select_fusion.1
  43.7 1.9 %fusion.95 = (f32[4,8,64]{2,1,0:T(8,128)S(1)}, f32[4,8,64,128]{3,2,1,0:T(8,128)S(1)}) fusion(bf16[4,8,64,128]{3,2,1,0:T(8,128)(2,1)} %param.5, bf16[4,8,1,128]{3,2,1,0:T(2,128)(2,1)S(1)} %get-tuple-element.62, bf16[4,8,63,128]{3,2,1,0:T(8,128)(2,1)S(1)} %slice.293, bf16[4,8,63,128]{3,2,1,0:T(8,128)(2,1)S(1)} %bitcast.366, ...), kind=kLoop, calls=%fused_computation.235 | loop fusion | flops 8386560 | bytes 4726784 | tf_op jit(solution)/shard_map/reduce_sum | solution.py:143
  45.7 11.2 %fusion.35 = (bf16[4,8,64,128]{3,2,1,0:T(8,128)(2,1)S(1)}, f32[4,8,64,128]{3,2,1,0:T(8,128)S(1)}, f32[4,8,64,128]{3,2,1,0:T(8,128)}) fusion(bf16[4,1,64,128]{3,2,1,0:T(8,128)(2,1)S(1)} %get-tuple-element.54, bf16[4,7,64,128]{3,2,1,0:T(8,128)(2,1)S(1)} %slice.287, bf16[4,7,64,128]{3,2,1,0:T(8,128)(2,1)S(1)} %slice.286, ...), kind=kOutput, calls=%fused_computation.73 | output fusion | flops 10225791 | bytes 7880704 | tf_op jit(solution)/shard_map/sub | solution.py:146
  56.9 0.8 multiply_convert_fusion.7
  57.6 0.6 multiply_convert_fusion.9
  58.3 0.7 fusion.31
  59.0 0.7 fusion.33
  60.1 0.8 collective-permute-start.7
  60.9 4.6 %collective-permute-start.8 = (bf16[4,1,64,128]{3,2,1,0:T(8,128)(2,1)S(1)}, bf16[4,1,64,128]{3,2,1,0:T(8,128)(2,1)S(1)}, u32[]{:S(2)}, u32[]{:S(2)}) collective-permute-start(bf16[4,1,64,128]{3,2,1,0:T(8,128)(2,1)S(1)} %get-tuple-element.33), channel_id=1, source_target_pairs={{0,2},{2,0},{4,6},{6,4},{1,3},{3,1},{5,7},{7,5},{8,10},{10,8},{12,... | collective-permute-start | bytes 196616 | tf_op jit(solution)/shard_map/ppermute | solution.py:72
  65.5 4.6 %collective-permute-start.5 = (bf16[1,8,64,128]{3,2,1,0:T(8,128)(2,1)S(1)}, bf16[1,8,64,128]{3,2,1,0:T(8,128)(2,1)S(1)}, u32[]{:S(2)}, u32[]{:S(2)}) collective-permute-start(bf16[1,8,64,128]{3,2,1,0:T(8,128)(2,1)S(1)} %get-tuple-element.36), channel_id=1, source_target_pairs={{8,16},{16,8},{24,32},{32,24},{40,48},{48,40},{56,64},{64,56},{72,... | collective-permute-start | bytes 393224 | tf_op jit(solution)/shard_map/ppermute | solution.py:76
  70.2 0.3 collective-permute-start.6
  70.6 2.2 %collective-permute-done.5 = bf16[1,8,64,128]{3,2,1,0:T(8,128)(2,1)S(1)} collective-permute-done((bf16[1,8,64,128]{3,2,1,0:T(8,128)(2,1)S(1)}, bf16[1,8,64,128]{3,2,1,0:T(8,128)(2,1)S(1)}, u32[]{:S(2)}, u32[]{:S(2)}) %collective-permute-start.5) | collective-permute-done | bytes 131104 | tf_op jit(solution)/shard_map/ppermute | solution.py:76
  73.3 0.2 fusion.77
  73.7 3.8 %fusion.1 = f32[6,4,8,64]{3,2,1,0:T(8,128)S(1)} fusion(bf16[6,4,8,64,128]{4,3,2,1,0:T(8,128)(2,1)S(1)} %fusion.77, f32[6,4,8,64,128]{4,3,2,1,0:T(8,128)S(1)} %bitcast.363, f32[6,4,8,64]{3,2,1,0:T(8,128)S(1)} %copy-done.28), kind=kLoop, calls=%fused_computation.5 | loop fusion | flops 6279168 | bytes 9535488 | tf_op jit(solution)/shard_map/reduce_sum | solution.py:156
  77.6 5.7 %fusion.15 = f32[6,128,128]{2,1,0:T(8,128)S(1)} fusion(bf16[6,4,8,64,128]{4,3,2,1,0:T(8,128)(2,1)S(1)} %copy-done.22, bf16[6,4,8,64,128]{4,3,2,1,0:T(8,128)(2,1)S(1)} %fusion.77, f32[6,4,8,64]{3,2,1,0:T(8,128)S(1)} %broadcast_multiply_fusion.1, f32[6,4,8,64]{3,2,1,0:T(8,128)S(1)} %copy-done.28), kind=kOutput, calls=%fused_computation.65 | convolution fusion | flops 408944640 | bytes 6782976 | tf_op jit(solution)/shard_map/dxyzk,dxyzl->dkl/dot_general | solution.py:158
  83.3 5.5 %fusion.89 = f32[6,4,8,64,128]{4,3,2,1,0:T(8,128)S(1)} fusion(bf16[6,128,128]{2,1,0:T(8,128)(2,1)S(1)} %copy-done.18, bf16[6,4,8,64,128]{4,3,2,1,0:T(8,128)(2,1)S(1)} %fusion.77, f32[6,4,8,64]{3,2,1,0:T(8,128)S(1)} %broadcast_multiply_fusion.1, f32[6,4,8,64]{3,2,1,0:T(8,128)S(1)} %copy-done.28), kind=kOutput, calls=%fused_computation.187 | convolution fusion | flops 408944640 | bytes 9732096 | tf_op jit(solution)/shard_map/dxyzl,dkl->dxyzk/dot_general | solution.py:161
  88.8 1.1 multiply_convert_fusion.2
  89.9 0.5 multiply_convert_fusion.1
  90.4 0.4 collective-permute-start.14
  90.8 1.0 multiply_convert_fusion.6
  91.8 1.2 multiply_convert_fusion.3
  93.4 0.8 collective-permute-start.12
  94.2 2.9 %collective-permute-start.13 = (bf16[4,1,64,128]{3,2,1,0:T(8,128)(2,1)S(1)}, bf16[4,1,64,128]{3,2,1,0:T(8,128)(2,1)S(1)}, u32[]{:S(2)}, u32[]{:S(2)}) collective-permute-start(bf16[4,1,64,128]{3,2,1,0:T(8,128)(2,1)S(1)} %get-tuple-element.27), channel_id=1, source_target_pairs={{0,2},{2,0},{4,6},{6,4},{1,3},{3,1},{5,7},{7,5},{8,10},{10,8},{12,... | collective-permute-start | bytes 196616 | tf_op jit(solution)/shard_map/ppermute | solution.py:72
  97.1 4.5 %collective-permute-start.10 = (bf16[1,8,64,128]{3,2,1,0:T(8,128)(2,1)S(1)}, bf16[1,8,64,128]{3,2,1,0:T(8,128)(2,1)S(1)}, u32[]{:S(2)}, u32[]{:S(2)}) collective-permute-start(bf16[1,8,64,128]{3,2,1,0:T(8,128)(2,1)S(1)} %get-tuple-element.30), channel_id=1, source_target_pairs={{8,16},{16,8},{24,32},{32,24},{40,48},{48,40},{56,64},{64,56},{72,... | collective-permute-start | bytes 393224 | tf_op jit(solution)/shard_map/ppermute | solution.py:76
  101.8 2.4 %collective-permute-done.10 = bf16[1,8,64,128]{3,2,1,0:T(8,128)(2,1)S(1)} collective-permute-done((bf16[1,8,64,128]{3,2,1,0:T(8,128)(2,1)S(1)}, bf16[1,8,64,128]{3,2,1,0:T(8,128)(2,1)S(1)}, u32[]{:S(2)}, u32[]{:S(2)}) %collective-permute-start.10) | collective-permute-done | bytes 131104 | tf_op jit(solution)/shard_map/ppermute | solution.py:76
  104.7 0.2 fusion.83
  105.0 3.8 %fusion.4 = f32[6,4,8,64]{3,2,1,0:T(8,128)S(1)} fusion(bf16[6,4,8,64,128]{4,3,2,1,0:T(8,128)(2,1)S(1)} %fusion.83, f32[6,4,8,64,128]{4,3,2,1,0:T(8,128)S(1)} %bitcast.365, f32[6,4,8,64]{3,2,1,0:T(8,128)S(1)} %broadcast_divide_fusion), kind=kLoop, calls=%fused_computation.8 | loop fusion | flops 6279168 | bytes 9535488 | tf_op jit(solution)/shard_map/reduce_sum | solution.py:156
  108.8 6.3 %fusion.25 = f32[6,128,128]{2,1,0:T(8,128)} fusion(f32[6,128,128]{2,1,0:T(8,128)S(1)} %fusion.15, bf16[6,4,8,64,128]{4,3,2,1,0:T(8,128)(2,1)S(1)} %copy-done.20, bf16[6,4,8,64,128]{4,3,2,1,0:T(8,128)(2,1)S(1)} %fusion.83, f32[6,4,8,64]{3,2,1,0:T(8,128)S(1)} %broadcast_multiply_fusion, f32[6,4,8,64]{3,2,1,0:T(8,128)S(1)} %broadcast_divide_fusion), kind=kOutput, calls=%fused_computation.67 | convolution fusion | flops 409042944 | bytes 7176192 | tf_op jit(solution)/shard_map/dxyzk,dxyzl->dkl/dot_general | solution.py:158
  115.1 20.9 %all-to-all-start = ((f32[256,1,384]{2,1,0:T(1,128)}), f32[256,1,384]{2,1,0:T(1,128)S(1)}, u32[]{:S(2)}, u32[]{:S(2)}) async-start(f32[256,1,384]{2,1,0:T(1,128)} %bitcast.75), calls=%async_computation | async-start | bytes 786432 | tf_op jit(solution)/shard_map/all_to_all | solution.py:191
  136.1 0.8 reshape.80
  137.0 17.5 %all-to-all-done = f32[256,1,384]{2,1,0:T(1,128)S(1)} async-done(((f32[256,1,384]{2,1,0:T(1,128)}), f32[256,1,384]{2,1,0:T(1,128)S(1)}, u32[]{:S(2)}, u32[]{:S(2)}) %all-to-all-start) | async-done | bytes 393248 | tf_op jit(solution)/shard_map/all_to_all | solution.py:191
  154.4 0.3 reduce_sum.69
  154.7 0.7 multiply_reduce_fusion
  155.5 1.0 broadcast_in_dim.27
  156.4 5.7 %all-to-all-start.1 = ((f32[256,1,384]{2,1,0:T(1,128)}), f32[256,1,384]{2,1,0:T(1,128)S(1)}, u32[]{:S(2)}, u32[]{:S(2)}) async-start(f32[256,1,384]{2,1,0:T(1,128)} %broadcast_in_dim.27), calls=%async_computation.1 | async-start | bytes 786432 | tf_op jit(solution)/shard_map/all_to_all | solution.py:194
  162.2 8.0 %fusion.85 = f32[6,4,8,64,128]{4,3,2,1,0:T(8,128)S(1)} fusion(bf16[6,128,128]{2,1,0:T(8,128)(2,1)S(1)} %copy-done.18, bf16[6,4,8,64,128]{4,3,2,1,0:T(8,128)(2,1)} %copy-done.10, f32[6,4,8,64]{3,2,1,0:T(8,128)S(1)} %broadcast_multiply_fusion, f32[6,4,8,64]{3,2,1,0:T(8,128)S(1)} %broadcast_divide_fusion), kind=kOutput, calls=%fused_computation.183 | convolution fusion | flops 408944640 | bytes 9732096 | tf_op jit(solution)/shard_map/dxyzl,dkl->dxyzk/dot_general | solution.py:161
  170.3 4.1 %fusion.50 = f32[4,8,64,128]{3,2,1,0:T(8,128)} fusion(f32[6,4,8,64,128]{4,3,2,1,0:T(8,128)S(1)} %fusion.85, f32[4,8,64,128]{3,2,1,0:T(8,128)S(1)} %get-tuple-element.7, f32[4,8,64,128]{3,2,1,0:T(8,128)} %get-tuple-element.65, bf16[4,8,64,128]{3,2,1,0:T(8,128)(2,1)S(1)} %copy-done.16, f32[4,8,64,128]{3,2,1,0:T(8,128)S(1)} %copy-done.9, ...), kind=kLoop, calls=%fused_computation.88 | loop fusion | flops 13893632 | bytes 19922944 | tf_op jit(solution)/shard_map/mul | solution.py:233
  174.4 6.2 %all-to-all-done.1 = f32[256,1,384]{2,1,0:T(1,128)S(1)} async-done(((f32[256,1,384]{2,1,0:T(1,128)}), f32[256,1,384]{2,1,0:T(1,128)S(1)}, u32[]{:S(2)}, u32[]{:S(2)}) %all-to-all-start.1) | async-done | bytes 393248 | tf_op jit(solution)/shard_map/all_to_all | solution.py:194
  180.6 0.7 copy.56
  (133 shorter events, 4.0 us)
Async XLA Ops:
  0.6 4.7 %copy-start = (bf16[6,4,8,64,128]{4,3,2,1,0:T(8,128)(2,1)S(1)}, bf16[6,4,8,64,128]{4,3,2,1,0:T(8,128)(2,1)}, u32[]{:S(2)}) copy-start(bf16[6,4,8,64,128]{4,3,2,1,0:T(8,128)(2,1)} %param.8) | copy-start | bytes 9437188
  5.6 1.9 %copy-start.4 = (bf16[6,4,8,64,128]{4,3,2,1,0:T(8,128)(2,1)S(1)}, bf16[6,4,8,64,128]{4,3,2,1,0:T(8,128)(2,1)}, u32[]{:S(2)}) copy-start(bf16[6,4,8,64,128]{4,3,2,1,0:T(8,128)(2,1)} %param.7) | copy-start | bytes 9437188
  7.7 1.0 copy-start.31
  9.5 23.4 %copy-start.17 = (bf16[6,128,128]{2,1,0:T(8,128)(2,1)}, bf16[6,128,128]{2,1,0:T(8,128)(2,1)S(1)}, u32[]{:S(2)}) copy-start(bf16[6,128,128]{2,1,0:T(8,128)(2,1)S(1)} %get-tuple-element.42) | copy-start | bytes 589828
  10.0 1.6 copy-start.19
  10.0 3.5 %copy-start.21 = (bf16[6,4,8,64,128]{4,3,2,1,0:T(8,128)(2,1)}, bf16[6,4,8,64,128]{4,3,2,1,0:T(8,128)(2,1)S(1)}, u32[]{:S(2)}) copy-start(bf16[6,4,8,64,128]{4,3,2,1,0:T(8,128)(2,1)S(1)} %get-tuple-element.69) | copy-start | bytes 9437188
  13.5 2.6 %copy-start.3 = (f32[6,4,8,64,128]{4,3,2,1,0:T(8,128)}, f32[6,4,8,64,128]{4,3,2,1,0:T(8,128)S(1)}, u32[]{:S(2)}) copy-start(f32[6,4,8,64,128]{4,3,2,1,0:T(8,128)S(1)} %get-tuple-element.64) | copy-start | bytes 18874372
  13.5 2.7 %copy-start.27 = (f32[6,4,8,64]{3,2,1,0:T(8,128)}, f32[6,4,8,64]{3,2,1,0:T(8,128)S(1)}, u32[]{:S(2)}) copy-start(f32[6,4,8,64]{3,2,1,0:T(8,128)S(1)} %broadcast_divide_fusion.1) | copy-start | bytes 147460
  16.2 1.9 %copy-start.12 = (bf16[6,4,8,64,128]{4,3,2,1,0:T(8,128)(2,1)}, bf16[6,4,8,64,128]{4,3,2,1,0:T(8,128)(2,1)S(1)}, u32[]{:S(2)}) copy-start(bf16[6,4,8,64,128]{4,3,2,1,0:T(8,128)(2,1)S(1)} %multiply_convert_fusion) | copy-start | bytes 9437188
  18.1 21.1 %copy-start.25 = (bf16[4,8,64,128]{3,2,1,0:T(8,128)(2,1)}, bf16[4,8,64,128]{3,2,1,0:T(8,128)(2,1)S(1)}, u32[]{:S(2)}) copy-start(bf16[4,8,64,128]{3,2,1,0:T(8,128)(2,1)S(1)} %get-tuple-element.22) | copy-start | bytes 1572868
  18.8 22.8 %collective-permute-start.4 = (bf16[4,8,1,128]{3,2,1,0:T(2,128)(2,1)}, bf16[4,8,1,128]{3,2,1,0:T(2,128)(2,1)S(1)}, u32[]{:S(2)}, u32[]{:S(2)}) collective-permute-start(bf16[4,8,1,128]{3,2,1,0:T(2,128)(2,1)} %broadcast_select_fusion.27), channel_id=1, source_target_pairs={{0,1},{1,0},{2,3},{3,2},{4,5},{5,4},{6,7},{7,6},{8,9},{9,8},{10,11... | collective-permute-start | bytes 24584 | tf_op jit(solution)/shard_map/ppermute | solution.py:72
  23.0 19.8 %collective-permute-start = (bf16[1,8,64,128]{3,2,1,0:T(8,128)(2,1)}, bf16[1,8,64,128]{3,2,1,0:T(8,128)(2,1)}, u32[]{:S(2)}, u32[]{:S(2)}) collective-permute-start(bf16[1,8,64,128]{3,2,1,0:T(8,128)(2,1)} %get-tuple-element.25), channel_id=1, source_target_pairs={{0,8},{8,0},{16,24},{24,16},{32,40},{40,32},{48,56},{56,48},{64,72... | collective-permute-start | bytes 393224 | tf_op jit(solution)/shard_map/ppermute | solution.py:72
  23.9 18.8 %collective-permute-start.1 = (bf16[1,8,64,128]{3,2,1,0:T(8,128)(2,1)}, bf16[1,8,64,128]{3,2,1,0:T(8,128)(2,1)}, u32[]{:S(2)}, u32[]{:S(2)}) collective-permute-start(bf16[1,8,64,128]{3,2,1,0:T(8,128)(2,1)} %get-tuple-element.26), channel_id=1, source_target_pairs={{8,16},{16,8},{24,32},{32,24},{40,48},{48,40},{56,64},{64,56},{72,... | collective-permute-start | bytes 393224 | tf_op jit(solution)/shard_map/ppermute | solution.py:76
  28.5 13.2 %collective-permute-start.2 = (bf16[4,1,64,128]{3,2,1,0:T(8,128)(2,1)}, bf16[4,1,64,128]{3,2,1,0:T(8,128)(2,1)}, u32[]{:S(2)}, u32[]{:S(2)}) collective-permute-start(bf16[4,1,64,128]{3,2,1,0:T(8,128)(2,1)} %get-tuple-element.37), channel_id=1, source_target_pairs={{0,2},{2,0},{4,6},{6,4},{1,3},{3,1},{5,7},{7,5},{8,10},{10,8},{12,... | collective-permute-start | bytes 196616 | tf_op jit(solution)/shard_map/ppermute | solution.py:72
  29.7 11.9 %collective-permute-start.3 = (bf16[4,1,64,128]{3,2,1,0:T(8,128)(2,1)}, bf16[4,1,64,128]{3,2,1,0:T(8,128)(2,1)}, u32[]{:S(2)}, u32[]{:S(2)}) collective-permute-start(bf16[4,1,64,128]{3,2,1,0:T(8,128)(2,1)} %get-tuple-element.38), channel_id=1, source_target_pairs={{2,4},{4,2},{3,5},{5,3},{10,12},{12,10},{11,13},{13,11},{18,20},{2... | collective-permute-start | bytes 196616 | tf_op jit(solution)/shard_map/ppermute | solution.py:76
  41.6 4.1 %copy-start.11 = (bf16[3,8,64,128]{3,2,1,0:T(8,128)(2,1)S(1)}, bf16[3,8,64,128]{3,2,1,0:T(8,128)(2,1)}, u32[]{:S(2)}) copy-start(bf16[3,8,64,128]{3,2,1,0:T(8,128)(2,1)} %get-tuple-element.23) | copy-start | bytes 1179652
  41.6 4.1 %copy-start.15 = (bf16[4,8,64,128]{3,2,1,0:T(8,128)(2,1)S(1)}, bf16[4,8,64,128]{3,2,1,0:T(8,128)(2,1)}, u32[]{:S(2)}) copy-start(bf16[4,8,64,128]{3,2,1,0:T(8,128)(2,1)} %param.5) | copy-start | bytes 1572868
  41.6 4.1 %copy-start.30 = (f32[4,8,64,128]{3,2,1,0:T(8,128)S(1)}, f32[4,8,64,128]{3,2,1,0:T(8,128)}, u32[]{:S(2)}) copy-start(f32[4,8,64,128]{3,2,1,0:T(8,128)} %param.9) | copy-start | bytes 3145732
  45.6 11.3 %copy-start.8 = (f32[4,8,64,128]{3,2,1,0:T(8,128)}, f32[4,8,64,128]{3,2,1,0:T(8,128)S(1)}, u32[]{:S(2)}) copy-start(f32[4,8,64,128]{3,2,1,0:T(8,128)S(1)} %get-tuple-element.13) | copy-start | bytes 3145732
  58.3 1.6 copy-start.26
  58.9 0.9 copy-start.24
  59.0 14.5 %slice-start = ((s8[6291456]{0:T(1024)(128)(4,1)}), s8[4194304]{0:T(1024)(128)(4,1)S(1)}, s32[]{:S(2)}) async-start(s8[6291456]{0:T(1024)(128)(4,1)} %bitcast.362), calls=%async_computation.2 | async-start | bytes 8388608
  59.7 10.8 %collective-permute-start.9 = (bf16[4,8,1,128]{3,2,1,0:T(2,128)(2,1)S(1)}, bf16[4,8,1,128]{3,2,1,0:T(2,128)(2,1)S(1)}, u32[]{:S(2)}, u32[]{:S(2)}) collective-permute-start(bf16[4,8,1,128]{3,2,1,0:T(2,128)(2,1)S(1)} %broadcast_select_fusion.24), channel_id=1, source_target_pairs={{0,1},{1,0},{2,3},{3,2},{4,5},{5,4},{6,7},{7,6},{8,9},{9,8},{10,11... | collective-permute-start | bytes 24584 | tf_op jit(solution)/shard_map/ppermute | solution.py:72
  59.8 13.1 %slice-start.6 = ((bf16[4,8,64,128]{3,2,1,0:T(8,128)(2,1)}), bf16[4,7,64,128]{3,2,1,0:T(8,128)(2,1)S(1)}, s32[]{:S(2)}) async-start(bf16[4,8,64,128]{3,2,1,0:T(8,128)(2,1)} %copy-done.26), calls=%async_computation.8 | async-start | bytes 917504 | tf_op jit(solution)/shard_map/slice | solution.py:128
  59.9 13.0 %slice-start.5 = ((bf16[4,8,64,128]{3,2,1,0:T(8,128)(2,1)}), bf16[3,8,64,128]{3,2,1,0:T(8,128)(2,1)S(1)}, s32[]{:S(2)}) async-start(bf16[4,8,64,128]{3,2,1,0:T(8,128)(2,1)} %copy-done.24), calls=%async_computation.7 | async-start | bytes 786432 | tf_op jit(solution)/shard_map/slice | solution.py:133
  59.9 13.6 %slice-start.1 = ((s8[6291456]{0:T(1024)(128)(4,1)}), s8[2097152]{0:T(1024)(128)(4,1)S(1)}, s32[]{:S(2)}) async-start(s8[6291456]{0:T(1024)(128)(4,1)} %bitcast.362), calls=%async_computation.3 | async-start | bytes 4194304
  60.1 10.4 %collective-permute-start.7 = (bf16[4,1,64,128]{3,2,1,0:T(8,128)(2,1)S(1)}, bf16[4,1,64,128]{3,2,1,0:T(8,128)(2,1)S(1)}, u32[]{:S(2)}, u32[]{:S(2)}) collective-permute-start(bf16[4,1,64,128]{3,2,1,0:T(8,128)(2,1)S(1)} %get-tuple-element.34), channel_id=1, source_target_pairs={{2,4},{4,2},{3,5},{5,3},{10,12},{12,10},{11,13},{13,11},{18,20},{2... | collective-permute-start | bytes 196616 | tf_op jit(solution)/shard_map/ppermute | solution.py:76
  60.9 9.6 %collective-permute-start.8 = (bf16[4,1,64,128]{3,2,1,0:T(8,128)(2,1)S(1)}, bf16[4,1,64,128]{3,2,1,0:T(8,128)(2,1)S(1)}, u32[]{:S(2)}, u32[]{:S(2)}) collective-permute-start(bf16[4,1,64,128]{3,2,1,0:T(8,128)(2,1)S(1)} %get-tuple-element.33), channel_id=1, source_target_pairs={{0,2},{2,0},{4,6},{6,4},{1,3},{3,1},{5,7},{7,5},{8,10},{10,8},{12,... | collective-permute-start | bytes 196616 | tf_op jit(solution)/shard_map/ppermute | solution.py:72
  65.5 7.3 %collective-permute-start.5 = (bf16[1,8,64,128]{3,2,1,0:T(8,128)(2,1)S(1)}, bf16[1,8,64,128]{3,2,1,0:T(8,128)(2,1)S(1)}, u32[]{:S(2)}, u32[]{:S(2)}) collective-permute-start(bf16[1,8,64,128]{3,2,1,0:T(8,128)(2,1)S(1)} %get-tuple-element.36), channel_id=1, source_target_pairs={{8,16},{16,8},{24,32},{32,24},{40,48},{48,40},{56,64},{64,56},{72,... | collective-permute-start | bytes 393224 | tf_op jit(solution)/shard_map/ppermute | solution.py:76
  70.2 2.6 %collective-permute-start.6 = (bf16[1,8,64,128]{3,2,1,0:T(8,128)(2,1)S(1)}, bf16[1,8,64,128]{3,2,1,0:T(8,128)(2,1)S(1)}, u32[]{:S(2)}, u32[]{:S(2)}) collective-permute-start(bf16[1,8,64,128]{3,2,1,0:T(8,128)(2,1)S(1)} %get-tuple-element.35), channel_id=1, source_target_pairs={{0,8},{8,0},{16,24},{24,16},{32,40},{40,32},{48,56},{56,48},{64,72... | collective-permute-start | bytes 393224 | tf_op jit(solution)/shard_map/ppermute | solution.py:72
  72.8 0.9 copy-start.28
  73.7 3.8 %copy-start.22 = (bf16[6,4,8,64,128]{4,3,2,1,0:T(8,128)(2,1)S(1)}, bf16[6,4,8,64,128]{4,3,2,1,0:T(8,128)(2,1)}, u32[]{:S(2)}) copy-start(bf16[6,4,8,64,128]{4,3,2,1,0:T(8,128)(2,1)} %copy-done.21) | copy-start | bytes 9437188
  77.6 5.7 %copy-start.18 = (bf16[6,128,128]{2,1,0:T(8,128)(2,1)S(1)}, bf16[6,128,128]{2,1,0:T(8,128)(2,1)}, u32[]{:S(2)}) copy-start(bf16[6,128,128]{2,1,0:T(8,128)(2,1)} %copy-done.17) | copy-start | bytes 589828
  83.2 5.5 %copy-start.1 = (bf16[6,4,8,64,128]{4,3,2,1,0:T(8,128)(2,1)S(1)}, bf16[6,4,8,64,128]{4,3,2,1,0:T(8,128)(2,1)}, u32[]{:S(2)}) copy-start(bf16[6,4,8,64,128]{4,3,2,1,0:T(8,128)(2,1)} %param.8) | copy-start | bytes 9437188
  89.9 1.9 %copy-start.13 = (f32[4,8,64,128]{3,2,1,0:T(8,128)}, f32[4,8,64,128]{3,2,1,0:T(8,128)S(1)}, u32[]{:S(2)}) copy-start(f32[4,8,64,128]{3,2,1,0:T(8,128)S(1)} %get-tuple-element.5) | copy-start | bytes 3145732
  90.3 1.5 copy-start.6
  90.4 11.3 %collective-permute-start.14 = (bf16[4,8,1,128]{3,2,1,0:T(2,128)(2,1)S(1)}, bf16[4,8,1,128]{3,2,1,0:T(2,128)(2,1)S(1)}, u32[]{:S(2)}, u32[]{:S(2)}) collective-permute-start(bf16[4,8,1,128]{3,2,1,0:T(2,128)(2,1)S(1)} %broadcast_select_fusion.21), channel_id=1, source_target_pairs={{0,1},{1,0},{2,3},{3,2},{4,5},{5,4},{6,7},{7,6},{8,9},{9,8},{10,11... | collective-permute-start | bytes 24584 | tf_op jit(solution)/shard_map/ppermute | solution.py:72
  91.8 1.3 copy-start.23
  91.8 13.1 %slice-start.2 = ((s8[6291456]{0:T(1024)(128)(4,1)}), s8[2097152]{0:T(1024)(128)(4,1)S(1)}, s32[]{:S(2)}) async-start(s8[6291456]{0:T(1024)(128)(4,1)} %bitcast.364), calls=%async_computation.4 | async-start | bytes 4194304
  93.1 11.9 %slice-start.3 = ((s8[6291456]{0:T(1024)(128)(4,1)}), s8[4194304]{0:T(1024)(128)(4,1)S(1)}, s32[]{:S(2)}) async-start(s8[6291456]{0:T(1024)(128)(4,1)} %bitcast.364), calls=%async_computation.5 | async-start | bytes 8388608
  93.1 11.2 %slice-start.4 = ((bf16[4,8,64,128]{3,2,1,0:T(8,128)(2,1)}), bf16[3,8,64,128]{3,2,1,0:T(8,128)(2,1)S(1)}, s32[]{:S(2)}) async-start(bf16[4,8,64,128]{3,2,1,0:T(8,128)(2,1)} %copy-done.23), calls=%async_computation.6 | async-start | bytes 786432 | tf_op jit(solution)/shard_map/slice | solution.py:128
  93.4 8.4 %collective-permute-start.12 = (bf16[4,1,64,128]{3,2,1,0:T(8,128)(2,1)S(1)}, bf16[4,1,64,128]{3,2,1,0:T(8,128)(2,1)S(1)}, u32[]{:S(2)}, u32[]{:S(2)}) collective-permute-start(bf16[4,1,64,128]{3,2,1,0:T(8,128)(2,1)S(1)} %get-tuple-element.28), channel_id=1, source_target_pairs={{2,4},{4,2},{3,5},{5,3},{10,12},{12,10},{11,13},{13,11},{18,20},{2... | collective-permute-start | bytes 196616 | tf_op jit(solution)/shard_map/ppermute | solution.py:76
  94.2 7.6 %collective-permute-start.13 = (bf16[4,1,64,128]{3,2,1,0:T(8,128)(2,1)S(1)}, bf16[4,1,64,128]{3,2,1,0:T(8,128)(2,1)S(1)}, u32[]{:S(2)}, u32[]{:S(2)}) collective-permute-start(bf16[4,1,64,128]{3,2,1,0:T(8,128)(2,1)S(1)} %get-tuple-element.27), channel_id=1, source_target_pairs={{0,2},{2,0},{4,6},{6,4},{1,3},{3,1},{5,7},{7,5},{8,10},{10,8},{12,... | collective-permute-start | bytes 196616 | tf_op jit(solution)/shard_map/ppermute | solution.py:72
  97.1 7.1 %collective-permute-start.10 = (bf16[1,8,64,128]{3,2,1,0:T(8,128)(2,1)S(1)}, bf16[1,8,64,128]{3,2,1,0:T(8,128)(2,1)S(1)}, u32[]{:S(2)}, u32[]{:S(2)}) collective-permute-start(bf16[1,8,64,128]{3,2,1,0:T(8,128)(2,1)S(1)} %get-tuple-element.30), channel_id=1, source_target_pairs={{8,16},{16,8},{24,32},{32,24},{40,48},{48,40},{56,64},{64,56},{72,... | collective-permute-start | bytes 393224 | tf_op jit(solution)/shard_map/ppermute | solution.py:76
  101.6 2.6 %collective-permute-start.11 = (bf16[1,8,64,128]{3,2,1,0:T(8,128)(2,1)S(1)}, bf16[1,8,64,128]{3,2,1,0:T(8,128)(2,1)S(1)}, u32[]{:S(2)}, u32[]{:S(2)}) collective-permute-start(bf16[1,8,64,128]{3,2,1,0:T(8,128)(2,1)S(1)} %get-tuple-element.29), channel_id=1, source_target_pairs={{0,8},{8,0},{16,24},{24,16},{32,40},{40,32},{48,56},{56,48},{64,72... | collective-permute-start | bytes 393224 | tf_op jit(solution)/shard_map/ppermute | solution.py:72
  104.9 3.9 %copy-start.10 = (bf16[6,4,8,64,128]{4,3,2,1,0:T(8,128)(2,1)}, bf16[6,4,8,64,128]{4,3,2,1,0:T(8,128)(2,1)S(1)}, u32[]{:S(2)}) copy-start(bf16[6,4,8,64,128]{4,3,2,1,0:T(8,128)(2,1)S(1)} %fusion.83) | copy-start | bytes 9437188
  105.0 3.9 %copy-start.20 = (bf16[6,4,8,64,128]{4,3,2,1,0:T(8,128)(2,1)S(1)}, bf16[6,4,8,64,128]{4,3,2,1,0:T(8,128)(2,1)}, u32[]{:S(2)}) copy-start(bf16[6,4,8,64,128]{4,3,2,1,0:T(8,128)(2,1)} %copy-done.19) | copy-start | bytes 9437188
  108.8 27.3 %copy-start.29 = (f32[6,128,128]{2,1,0:T(8,128)S(1)}, f32[6,128,128]{2,1,0:T(8,128)}, u32[]{:S(2)}) copy-start(f32[6,128,128]{2,1,0:T(8,128)} %get-tuple-element.41) | copy-start | bytes 1179652
  115.1 39.3 %all-to-all-start = ((f32[256,1,384]{2,1,0:T(1,128)}), f32[256,1,384]{2,1,0:T(1,128)S(1)}, u32[]{:S(2)}, u32[]{:S(2)}) async-start(f32[256,1,384]{2,1,0:T(1,128)} %bitcast.75), calls=%async_computation | async-start | bytes 786432 | tf_op jit(solution)/shard_map/all_to_all | solution.py:191
  136.1 34.1 %copy-start.16 = (bf16[4,8,64,128]{3,2,1,0:T(8,128)(2,1)S(1)}, bf16[4,8,64,128]{3,2,1,0:T(8,128)(2,1)}, u32[]{:S(2)}) copy-start(bf16[4,8,64,128]{3,2,1,0:T(8,128)(2,1)} %param.5) | copy-start | bytes 1572868
  156.4 24.2 %all-to-all-start.1 = ((f32[256,1,384]{2,1,0:T(1,128)}), f32[256,1,384]{2,1,0:T(1,128)S(1)}, u32[]{:S(2)}, u32[]{:S(2)}) async-start(f32[256,1,384]{2,1,0:T(1,128)} %broadcast_in_dim.27), calls=%async_computation.1 | async-start | bytes 786432 | tf_op jit(solution)/shard_map/all_to_all | solution.py:194
  162.2 8.1 %copy-start.2 = (bf16[6,4,8,64,128]{4,3,2,1,0:T(8,128)(2,1)S(1)}, bf16[6,4,8,64,128]{4,3,2,1,0:T(8,128)(2,1)}, u32[]{:S(2)}) copy-start(bf16[6,4,8,64,128]{4,3,2,1,0:T(8,128)(2,1)} %param.8) | copy-start | bytes 9437188
  162.2 8.1 %copy-start.5 = (bf16[6,4,8,64,128]{4,3,2,1,0:T(8,128)(2,1)S(1)}, bf16[6,4,8,64,128]{4,3,2,1,0:T(8,128)(2,1)}, u32[]{:S(2)}) copy-start(bf16[6,4,8,64,128]{4,3,2,1,0:T(8,128)(2,1)} %param.7) | copy-start | bytes 9437188
  162.2 8.1 %copy-start.7 = (f32[4,8,64,128]{3,2,1,0:T(8,128)S(1)}, f32[4,8,64,128]{3,2,1,0:T(8,128)}, u32[]{:S(2)}) copy-start(f32[4,8,64,128]{3,2,1,0:T(8,128)} %copy-done.6) | copy-start | bytes 3145732
  162.2 8.1 %copy-start.9 = (f32[4,8,64,128]{3,2,1,0:T(8,128)S(1)}, f32[4,8,64,128]{3,2,1,0:T(8,128)}, u32[]{:S(2)}) copy-start(f32[4,8,64,128]{3,2,1,0:T(8,128)} %copy-done.8) | copy-start | bytes 3145732
  162.2 8.1 %copy-start.14 = (f32[4,8,64,128]{3,2,1,0:T(8,128)S(1)}, f32[4,8,64,128]{3,2,1,0:T(8,128)}, u32[]{:S(2)}) copy-start(f32[4,8,64,128]{3,2,1,0:T(8,128)} %copy-done.13) | copy-start | bytes 3145732
